TPU v7x, 256 devices: a whole 4x4x8 slice. The times are simulated.
256 devices in a mesh: gx: 16 (over z, core), gy: 4 (over x), gz: 4 (over y).
Axes of the slice: x: 4, y: 4, z: 8, core: 2. Of those that a mesh axis runs over, the one named last changes fastest.
Arguments:
- fields: float32 [5, 512, 256, 512], P(None, 'gx', 'gy', 'gz'), may hold values from -4 to 9
- viscous: float32 [5], replicated, may hold values from 1 to 8000
Outputs:
- updated: float32 [5, 512, 256, 512], P(None, 'gx', 'gy', 'gz')
All inputs are finite; a program needn't handle non-finite values.
Results may differ from a plain program's by a relative error of at most 0.0003.
Values sent between devices are 32-bit elements; how exact they have to be, the bound alone decides.
No kernel may reach another device: no remote copies, remote signals or barrier semaphores. Data moves between devices by JAX's collectives and lax.ppermute only.
A program may use at most 128 MiB of HBM per device.

v0:
```python
import math

import jax
import jax.numpy as jnp
from jax import lax
from jax.sharding import PartitionSpec as P

advect = 0.3
root_ratio = (-1.0 + math.sqrt(5.0) / 3.0) * 1.5
line_gain = (1.0 + root_ratio * root_ratio) / (1.0 - root_ratio * root_ratio)
highest = lax.Precision.HIGHEST


def extended(array, sides, width):
    for axis, dim in sides:
        peers, length = (lax.axis_size(axis), array.shape[dim])
        up = [(i, (i + 1) % peers) for i in range(peers)]
        down = [(j, i) for i, j in up]
        last = lax.slice_in_dim(array, length - width, length, axis=dim)
        leading = lax.slice_in_dim(array, 0, width, axis=dim)
        before = lax.ppermute(last, axis, up)
        after = lax.ppermute(leading, axis, down)
        array = jnp.concatenate([before, array, after], axis=dim)
    return array


def carried_in(part, axis, combine, identity, reverse):
    count = lax.axis_size(axis)
    place = lax.axis_index(axis)
    ahead = count - 1 - place if reverse else place
    gathered = jax.tree.map(lambda a: lax.all_gather(a, axis), part)
    state = jax.tree.map(lambda a, e: jnp.zeros_like(a) + jnp.asarray(e, a.dtype), part, identity)

    def one(hop, state):
        source = count - 1 - hop if reverse else hop
        return combine(
            state, jax.tree.map(lambda a: lax.dynamic_index_in_dim(a, source, 0, False), gathered)
        )

    return lax.fori_loop(0, ahead, one, state)


def signed_power(exponent):
    parity = jnp.mod(exponent, 2.0)
    return (1.0 - 2.0 * parity) * jnp.exp(exponent * math.log(abs(root_ratio)))


def pade_kernel(length):
    row_index = jnp.arange(length, dtype=jnp.float32)[:, None]
    col_index = jnp.arange(length, dtype=jnp.float32)[None, :]
    offset = jnp.mod(row_index - col_index, float(length))
    closing = 1.0 - signed_power(jnp.float32(length))
    return line_gain * (signed_power(offset) + signed_power(length - offset)) / closing


def compact_source(line_block):

    def shifted(offset):
        return jnp.roll(line_block, -offset, axis=1)

    return 7.0 / 9.0 * (shifted(1) - shifted(-1)) + 1.0 / 36.0 * (shifted(2) - shifted(-2))


def span_derivative(fields):
    padded = extended(fields, (("gz", 3),), 3)
    span_count = fields.shape[3]

    def shifted(offset):
        return padded[..., 3 + offset : 3 + offset + span_count]

    return (
        45.0 * (shifted(1) - shifted(-1))
        - 9.0 * (shifted(2) - shifted(-2))
        + (shifted(3) - shifted(-3))
    ) / 60.0


def combine_wall(earlier, later_pair):
    return (later_pair[1][:, None, None] * earlier[0] + later_pair[0], earlier[1] * later_pair[1])


def wall_carries(explicit, viscous):
    row_count = explicit.shape[2]
    total_rows = row_count * lax.axis_size("gy")
    diagonal = 1.0 + 2.0 * viscous

    def pivot_step(previous, unused):
        current = 1.0 / (diagonal - viscous * viscous * previous)
        return (current, current)

    _, pivots = lax.scan(pivot_step, jnp.zeros_like(viscous), None, length=total_rows)
    pivots = lax.dynamic_slice_in_dim(pivots, lax.axis_index("gy") * row_count, row_count, 0).T
    log_gain = jnp.log(viscous[:, None] * pivots)
    inclusive = jnp.cumsum(log_gain, axis=1)
    exclusive = inclusive - log_gain
    row_index = jnp.arange(row_count)[:, None]
    col_index = jnp.arange(row_count)[None, :]
    lower_mask = col_index <= row_index
    upper_mask = col_index >= row_index
    spread = inclusive[:, :, None] - inclusive[:, None, :]
    forward_table = jnp.where(
        lower_mask, pivots[:, None, :] * jnp.exp(jnp.where(lower_mask, spread, 0.0)), 0.0
    )
    eliminated_local = jnp.einsum("fik,fxkz->fxiz", forward_table, explicit, precision=highest)
    block_gain = jnp.exp(inclusive[:, -1])
    zero_line = jnp.zeros_like(eliminated_local[:, :, -1])
    enter_low, _ = carried_in(
        (eliminated_local[:, :, -1], block_gain),
        "gy",
        combine_wall,
        (zero_line, jnp.ones_like(block_gain)),
        False,
    )
    eliminated = eliminated_local + jnp.exp(inclusive)[:, None, :, None] * enter_low[:, :, None, :]
    reach_log = exclusive[:, None, :] - exclusive[:, :, None]
    backward_table = jnp.where(upper_mask, jnp.exp(jnp.where(upper_mask, reach_log, 0.0)), 0.0)
    solved = jnp.einsum("fik,fxkz->fxiz", backward_table, eliminated, precision=highest)
    enter_high, _ = carried_in(
        (solved[:, :, 0], block_gain),
        "gy",
        combine_wall,
        (zero_line, jnp.ones_like(block_gain)),
        True,
    )
    trailing = jnp.exp(inclusive[:, -1:] - exclusive)
    return solved + trailing[:, None, :, None] * enter_high[:, :, None, :]


def shards(fields, viscous):
    span_slope = span_derivative(fields)
    line_block = lax.all_to_all(fields, "gx", split_axis=2, concat_axis=1, tiled=True)
    source = compact_source(line_block)
    kernel = pade_kernel(line_block.shape[1])
    derivative = jnp.einsum("ij,fjyz->fiyz", kernel, source, precision=highest)
    line_slope = lax.all_to_all(derivative, "gx", split_axis=1, concat_axis=2, tiled=True)
    explicit = fields - advect * fields[0] * line_slope - advect * fields[2] * span_slope
    updated = wall_carries(explicit, viscous)
    return updated


def solution(mesh):
    in_specs = (P(None, "gx", "gy", "gz"), P())
    out_specs = P(None, "gx", "gy", "gz")
    return jax.shard_map(shards, mesh=mesh, in_specs=in_specs, out_specs=out_specs, check_vma=False)
```

profile of v0, /device:TPU:24, one launch (start us, length us, event | category | flops | bytes accessed | tf_op | source)
XLA Modules:
  0.0 382.1 jit_solution(1591634177057598161)
XLA Ops:
  0.0 7.9 %copy.24 = f32[5,32,64,128]{3,1,0,2:T(8,128)} copy(f32[5,32,64,128]{3,2,1,0:T(8,128)} %param.8) | data formatting | bytes 10485760 | tf_op args[0]
  7.9 8.6 %all-to-all-start = ((f32[5,32,64,128]{3,1,0,2:T(8,128)}), f32[5,32,64,128]{3,1,0,2:T(8,128)}, u32[]{:S(2)}, u32[]{:S(2)}) async-start(f32[5,32,64,128]{3,1,0,2:T(8,128)} %copy.24), calls=%async_computation | async-start | bytes 10485760 | tf_op jit(solution)/shard_map/all_to_all | solution.py:131
  16.5 9.8 %fusion.126 = (f32[5,32,64,3]{3,2,1,0:T(8,128)}, f32[5,32,64,3]{3,2,1,0:T(8,128)}) fusion(f32[5,32,64,128]{3,2,1,0:T(8,128)} %param.8), kind=kLoop, calls=%fused_computation.140 | loop fusion | bytes 491520 | tf_op jit(solution)/shard_map/slice | solution.py:20
  26.4 3.5 copy.48
  29.8 0.8 collective-permute-start
  30.6 3.4 copy.49
  34.1 2.7 collective-permute-start.1
  36.8 0.0 copy-done.2
  36.8 96.5 %all-to-all-done = f32[5,32,64,128]{3,1,0,2:T(8,128)} async-done(((f32[5,32,64,128]{3,1,0,2:T(8,128)}), f32[5,32,64,128]{3,1,0,2:T(8,128)}, u32[]{:S(2)}, u32[]{:S(2)}) %all-to-all-start) | async-done | bytes 5242912 | tf_op jit(solution)/shard_map/all_to_all | solution.py:131
  133.3 3.3 copy.26
  136.7 3.3 fusion.123
  140.0 4.9 %fusion.125 = (f32[5,511,4,128]{3,1,2,0:T(8,128)}, f32[5,511,4,128]{3,1,2,0:T(8,128)}) fusion(f32[5,512,4,128]{3,1,2,0:T(8,128)S(1)} %bitcast.61), kind=kLoop, calls=%fused_computation.139 | loop fusion | bytes 20930560 | tf_op jit(solution)/shard_map/jit(_roll_static)/slice | solution.py:59
  144.9 27.7 %fusion.41 = f32[5,512,4,128]{1,3,2,0:T(8,128)} fusion(f32[5,1,4,128]{3,1,2,0:T(1,128)S(1)} %get-tuple-element.258, f32[5,511,4,128]{3,1,2,0:T(8,128)} %get-tuple-element.260, f32[5,511,4,128]{3,1,2,0:T(8,128)} %get-tuple-element.259, f32[5,1,4,128]{3,1,2,0:T(1,128)S(1)} %get-tuple-element.257, f32[5,2,4,128]{3,1,2,0:T(2,128)S(1)} %get-tuple-element.254, ...), kind=kOutput, calls=%fused_computation.57 | convolution fusion | flops 8072724480 | bytes 26214400 | tf_op jit(solution)/shard_map/ij,fjyz->fiyz/dot_general | solution.py:134
  172.6 7.3 %copy.28 = f32[5,512,4,128]{3,2,0,1:T(4,128)} copy(f32[5,512,4,128]{1,3,2,0:T(8,128)} %fusion.41) | data formatting | bytes 10485760 | tf_op jit(solution)/shard_map/ij,fjyz->fiyz/transpose | solution.py:134
  179.9 4.9 %all-to-all-start.1 = ((f32[5,512,4,128]{3,2,0,1:T(4,128)}), f32[5,512,4,128]{3,2,0,1:T(4,128)}, u32[]{:S(2)}, u32[]{:S(2)}) async-start(f32[5,512,4,128]{3,2,0,1:T(4,128)} %copy.28), calls=%async_computation.1 | async-start | bytes 10485760 | tf_op jit(solution)/shard_map/all_to_all | solution.py:135
  184.8 18.1 %while.43 = (s32[]{:T(128)}, f32[5]{0:T(128)S(1)}, f32[256,5]{1,0:T(8,128)S(1)}, f32[5]{0:T(128)S(1)}, f32[5]{0:T(128)S(1)}, /*index=5*/s32[]{:T(128)}, s32[]{:T(128)}) while((s32[]{:T(128)}, f32[5]{0:T(128)S(1)}, f32[256,5]{1,0:T(8,128)S(1)}, f32[5]{0:T(128)S(1)}, f32[5]{0:T(128)S(1)}, /*index=5*/s32[]{:T(128)}, s32[]{:T(128)}) %tuple.80), condition=%wide.region_1.2_spmd.clone, body=%wide.region_0.1_spmd.clone.sunk | while | flops 23 | bytes 211 | solution.py:91
  202.9 0.1 copy.39
  202.9 0.1 multiply_log_fusion
  203.0 0.2 reduce_window_sum.11
  203.2 0.2 slice_reduce_fusion
  203.4 0.1 subtract_exponential_fusion
  203.5 1.8 multiply_bitcast_fusion.1
  205.3 0.0 copy-start.3
  205.3 7.8 %copy.31 = f32[5,32,64,128]{3,1,2,0:T(8,128)} copy(f32[5,32,64,128]{3,2,1,0:T(8,128)} %param.8) | data formatting | bytes 10485760 | tf_op args[0]
  213.1 1.6 copy.23
  214.7 1.6 copy.38
  216.3 0.0 copy-done.3
  216.3 0.6 dynamic-slice
  217.5 0.2 dynamic-update-slice
  217.8 10.5 %all-reduce = f32[20]{0:T(128)S(1)} all-reduce(f32[20]{0:T(128)S(1)} %dynamic-update-slice), channel_id=2, replica_groups=mesh['gx'=16,'gy'=4,'gz'=4] {'gy'}, use_global_device_ids=true, to_apply=%add | all-reduce | flops 20 | bytes 160
  228.2 0.1 reshape.29
  228.3 0.0 collective-permute-done
  228.4 3.6 copy.34
  232.0 0.0 collective-permute-done.1
  232.0 3.5 copy.36
  235.5 66.1 %all-to-all-done.1 = f32[5,512,4,128]{3,2,0,1:T(4,128)} async-done(((f32[5,512,4,128]{3,2,0,1:T(4,128)}), f32[5,512,4,128]{3,2,0,1:T(4,128)}, u32[]{:S(2)}, u32[]{:S(2)}) %all-to-all-start.1) | async-done | bytes 5242912 | tf_op jit(solution)/shard_map/all_to_all | solution.py:135
  301.6 3.2 copy.29
  304.8 0.0 slice-start.1
  304.8 0.0 slice-start.3
  304.8 0.0 slice-start.5
  304.9 3.3 copy.30
  308.2 0.0 slice-done
  308.2 0.0 slice-done.2
  308.2 1.5 slice-done.4
  309.7 0.4 slice-done.1
  310.1 0.3 slice-done.3
  310.4 0.3 slice-done.5
  310.7 17.7 %fusion.9 = f32[5,32,64,128]{3,1,2,0:T(8,128)} fusion(f32[5,32,64,3]{3,1,2,0:T(8,128)S(1)} %bitcast.69, f32[5,32,64,128]{3,1,2,0:T(8,128)S(1)} %bitcast.65, f32[5,32,64,3]{3,1,2,0:T(8,128)S(1)} %bitcast.67, f32[5,32,64,128]{3,1,2,0:T(8,128)} %bitcast.70, f32[32,64,128]{2,0,1:T(8,128)} %copy.38, f32[32,64,128]{2,0,1:T(8,128)} %copy.23), kind=kLoop, calls=%fused_computation.22 | loop fusion | flops 22282240 | bytes 18071552 | tf_op jit(solution)/shard_map/sub | solution.py:136
  328.4 9.1 %fusion.47 = f32[5,32,64,128]{3,2,1,0:T(8,128)S(1)} fusion(f32[5,32,64,128]{3,1,2,0:T(8,128)} %fusion.9, f32[5,64]{1,0:T(8,128)S(1)} %reduce_window_sum.11, f32[5,64]{1,0:T(8,128)S(1)} %get-tuple-element.250, pred[64,64]{1,0:T(8,128)(4,1)S(1)} %iota_compare_fusion.1), kind=kOutput, calls=%fused_computation.59 | convolution fusion | flops 1006714880 | bytes 10492416 | tf_op jit(solution)/shard_map/fik,fxkz->fxiz/dot_general | solution.py:104
  337.5 0.0 copy-start.1
  337.5 2.3 copy-done.1
  339.8 0.1 slice.115
  339.9 12.7 %all-gather.1 = f32[20,32,1,128]{3,1,2,0:T(8,128)S(1)} all-gather(f32[5,32,1,128]{3,1,2,0:T(8,128)S(1)} %bitcast.74), channel_id=3, replica_groups=mesh['gx'=16,'gy'=4,'gz'=4] {'gy'}, dimensions={0}, use_global_device_ids=true | all-gather | bytes 409600 | tf_op jit(solution)/shard_map/all_gather | solution.py:31
  352.7 0.2 while.41
  352.9 7.6 %fusion.44 = f32[5,32,64,128]{3,2,1,0:T(8,128)S(1)} fusion(f32[5,32,64,128]{3,2,1,0:T(8,128)} %copy-done.1, f32[5,32,128]{2,1,0:T(8,128)S(1)} %get-tuple-element.195, f32[5,64]{1,0:T(8,128)S(1)} %get-tuple-element.263, f32[5,64]{1,0:T(8,128)S(1)} %get-tuple-element.248, pred[64,64]{1,0:T(8,128)(4,1)S(1)} %iota_compare_fusion), kind=kOutput, calls=%fused_computation.58 | convolution fusion | flops 1009315840 | bytes 10574336 | tf_op jit(solution)/shard_map/fik,fxkz->fxiz/dot_general | solution.py:117
  360.5 0.0 copy-start
  360.5 2.3 copy-done
  362.8 0.1 slice.116
  362.9 12.4 %all-gather.2 = f32[20,32,1,128]{3,1,2,0:T(8,128)S(1)} all-gather(f32[5,32,1,128]{3,1,2,0:T(8,128)S(1)} %bitcast.75), channel_id=4, replica_groups=mesh['gx'=16,'gy'=4,'gz'=4] {'gy'}, dimensions={0}, use_global_device_ids=true | all-gather | bytes 409600 | tf_op jit(solution)/shard_map/all_gather | solution.py:31
  375.3 0.4 while.42
  375.4 0.1 bitcast_add_fusion.5
  375.5 0.1 bitcast_add_fusion.5
  375.6 0.1 bitcast_add_fusion.5
  375.7 6.2 %multiply_add_fusion = f32[5,32,64,128]{3,2,1,0:T(8,128)} fusion(f32[5,32,64,128]{3,2,1,0:T(8,128)} %copy-done, f32[5,32,128]{2,1,0:T(8,128)S(1)} %get-tuple-element.196, f32[5,64]{1,0:T(8,128)S(1)} %get-tuple-element.247), kind=kLoop, calls=%fused_computation.49 | loop fusion | flops 2621440 | bytes 10568960 | tf_op jit(solution)/shard_map/add | solution.py:126
  (532 shorter events, 13.6 us)
Async XLA Ops:
  7.9 125.4 %all-to-all-start = ((f32[5,32,64,128]{3,1,0,2:T(8,128)}), f32[5,32,64,128]{3,1,0,2:T(8,128)}, u32[]{:S(2)}, u32[]{:S(2)}) async-start(f32[5,32,64,128]{3,1,0,2:T(8,128)} %copy.24), calls=%async_computation | async-start | bytes 10485760 | tf_op jit(solution)/shard_map/all_to_all | solution.py:131
  26.4 10.5 %copy-start.2 = (f32[5]{0:T(128)S(1)}, f32[5]{0:T(128)}, u32[]{:S(2)}) copy-start(f32[5]{0:T(128)} %param.9) | copy-start | bytes 64
  29.8 198.5 %collective-permute-start = (f32[5,32,64,3]{2,1,3,0:T(8,128)S(1)}, f32[5,32,64,3]{2,1,3,0:T(8,128)S(1)}, u32[]{:S(2)}, u32[]{:S(2)}) collective-permute-start(f32[5,32,64,3]{2,1,3,0:T(8,128)S(1)} %copy.48), channel_id=1, source_target_pairs={{1,0},{2,1},{3,2},{0,3},{5,4},{6,5},{7,6},{4,7},{9,8},{10,9},{11,1... | collective-permute-start | bytes 368648 | tf_op jit(solution)/shard_map/ppermute | solution.py:22
  34.1 197.9 %collective-permute-start.1 = (f32[5,32,64,3]{2,1,3,0:T(8,128)S(1)}, f32[5,32,64,3]{2,1,3,0:T(8,128)S(1)}, u32[]{:S(2)}, u32[]{:S(2)}) collective-permute-start(f32[5,32,64,3]{2,1,3,0:T(8,128)S(1)} %copy.49), channel_id=1, source_target_pairs={{0,1},{1,2},{2,3},{3,0},{4,5},{5,6},{6,7},{7,4},{8,9},{9,10},{10,1... | collective-permute-start | bytes 368648 | tf_op jit(solution)/shard_map/ppermute | solution.py:21
  179.9 121.7 %all-to-all-start.1 = ((f32[5,512,4,128]{3,2,0,1:T(4,128)}), f32[5,512,4,128]{3,2,0,1:T(4,128)}, u32[]{:S(2)}, u32[]{:S(2)}) async-start(f32[5,512,4,128]{3,2,0,1:T(4,128)} %copy.28), calls=%async_computation.1 | async-start | bytes 10485760 | tf_op jit(solution)/shard_map/all_to_all | solution.py:135
  205.3 11.0 %copy-start.3 = (u32[256]{0:T(256)S(1)}, u32[256]{0:T(256)}, u32[]{:S(2)}) copy-start(u32[256]{0:T(256)} %constant.139) | copy-start | bytes 3076
  301.6 6.6 %slice-start = ((s8[5242880]{0:T(1024)(128)(4,1)}), s8[4194304]{0:T(1024)(128)(4,1)S(1)}, s32[]{:S(2)}) async-start(s8[5242880]{0:T(1024)(128)(4,1)} %bitcast.64), calls=%async_computation.2 | async-start | bytes 8388608
  301.6 6.6 %slice-start.2 = ((s8[5242880]{0:T(1024)(128)(4,1)}), s8[4194304]{0:T(1024)(128)(4,1)S(1)}, s32[]{:S(2)}) async-start(s8[5242880]{0:T(1024)(128)(4,1)} %bitcast.66), calls=%async_computation.4 | async-start | bytes 8388608
  301.6 8.1 %slice-start.4 = ((s8[5242880]{0:T(1024)(128)(4,1)}), s8[4194304]{0:T(1024)(128)(4,1)S(1)}, s32[]{:S(2)}) async-start(s8[5242880]{0:T(1024)(128)(4,1)} %bitcast.68), calls=%async_computation.6 | async-start | bytes 8388608
  304.8 5.3 %slice-start.1 = ((s8[5242880]{0:T(1024)(128)(4,1)}), s8[1048576]{0:T(1024)(128)(4,1)S(1)}, s32[]{:S(2)}) async-start(s8[5242880]{0:T(1024)(128)(4,1)} %bitcast.64), calls=%async_computation.3 | async-start | bytes 2097152
  304.8 5.6 %slice-start.3 = ((s8[5242880]{0:T(1024)(128)(4,1)}), s8[1048576]{0:T(1024)(128)(4,1)S(1)}, s32[]{:S(2)}) async-start(s8[5242880]{0:T(1024)(128)(4,1)} %bitcast.66), calls=%async_computation.5 | async-start | bytes 2097152
  304.8 5.9 %slice-start.5 = ((s8[5242880]{0:T(1024)(128)(4,1)}), s8[1048576]{0:T(1024)(128)(4,1)S(1)}, s32[]{:S(2)}) async-start(s8[5242880]{0:T(1024)(128)(4,1)} %bitcast.68), calls=%async_computation.7 | async-start | bytes 2097152
  337.5 2.4 copy-start.1
  360.5 2.4 copy-start
where the time goes:
time: 389 us; the launch traced here: 382 us
  waiting for transfers between devices  163 us (42%)
  local copies, waits for them, and re-layouts  86.5 us (22%)
  matrix products  44.4 us (11%)
  blocking collectives  35.6 us (9%)
  other arithmetic  30 us (8%)
  starting transfers between devices  17 us (4%)
  loops' own time  4.92 us (1%)
    all_to_all x1, waiting for transfers between devices, shards(): lax.all_to_all(fields, 'gx', split_axis=2, concat_axis=1, tiled=True)  96.5 us
    all_to_all x1, waiting for transfers between devices, shards(): lax.all_to_all(derivative, 'gx', split_axis=1, concat_axis=2, tiled=True)  66.1 us
    unnamed x27, local copies, waits for them, and re-layouts  30.7 us
    dot_general x1, matrix products, shards(): derivative = jnp.einsum('ij,fjyz->fiyz', kernel, source, precision=highest)  27.7 us
    all_gather x2, blocking collectives, carried_in(): gathered = jax.tree.map(lambda a: lax.all_gather(a, axis), part)  25.1 us
    sub x1, other arithmetic, shards(): fields - advect * fields[0] * line_slope - advect * fields[2] * span_slope  17.7 us
    unnamed x1, blocking collectives  10.5 us
    slice x1, local copies, waits for them, and re-layouts, extended(): leading = lax.slice_in_dim(array, 0, width, axis=dim)  9.83 us
  transfers between devices with their start and end apart: 4, of which 2 were waited for; matrix products, arithmetic and copies ran while one was open for 26% of the time, Pallas kernels for 0%

commit v1 on v0

--- a/solution.py
+++ b/solution.py
@@ -126,13 +126,47 @@
     return solved + trailing[:, None, :, None] * enter_high[:, :, None, :]
 
 
+def shifted_in(array, axis, shift):
+    peers = lax.axis_size(axis)
+    return lax.ppermute(array, axis, [(i, (i + shift) % peers) for i in range(peers)])
+
+
+def line_derivative(fields):
+    peers = lax.axis_size("gx")
+    length = fields.shape[1]
+    total = length * peers
+    padded = extended(fields, (("gx", 1),), 2)
+
+    def plane(offset):
+        return padded[:, 2 + offset : 2 + offset + length]
+
+    source = 7.0 / 9.0 * (plane(1) - plane(-1)) + 1.0 / 36.0 * (plane(2) - plane(-2))
+    index = jnp.arange(length, dtype=jnp.float32)
+    distance = jnp.abs(index[:, None] - index[None, :])
+    near = signed_power(distance)
+    ends = jnp.stack([signed_power(length - 1 - index), signed_power(index)])
+    moments = jnp.einsum("mj,fjyz->fmyz", ends, source, precision=highest)
+    local = jnp.einsum("ij,fjyz->fiyz", near, source, precision=highest)
+    block_weight = root_ratio**length
+    left = shifted_in(moments[:, 0], "gx", 1) + block_weight * shifted_in(moments[:, 0], "gx", 2)
+    right = shifted_in(moments[:, 1], "gx", -1) + block_weight * shifted_in(moments[:, 1], "gx", -2)
+    span = 2
+    while span < peers:
+        weight = root_ratio ** (length * span)
+        left = left + weight * shifted_in(left, "gx", span)
+        right = right + weight * shifted_in(right, "gx", -span)
+        span *= 2
+    wrap = root_ratio / (1.0 - root_ratio**total)
+    rising = signed_power(index)[None, :, None, None]
+    falling = signed_power(length - 1 - index)[None, :, None, None]
+    return line_gain * (
+        local + wrap * (rising * left[:, None] + falling * right[:, None])
+    )
+
+
 def shards(fields, viscous):
     span_slope = span_derivative(fields)
-    line_block = lax.all_to_all(fields, "gx", split_axis=2, concat_axis=1, tiled=True)
-    source = compact_source(line_block)
-    kernel = pade_kernel(line_block.shape[1])
-    derivative = jnp.einsum("ij,fjyz->fiyz", kernel, source, precision=highest)
-    line_slope = lax.all_to_all(derivative, "gx", split_axis=1, concat_axis=2, tiled=True)
+    line_slope = line_derivative(fields)
     explicit = fields - advect * fields[0] * line_slope - advect * fields[2] * span_slope
     updated = wall_carries(explicit, viscous)
     return updated

time: 389 us -> 236 us (0.61)
  waiting for transfers between devices: 163 us -> 24 us
  local copies, waits for them, and re-layouts: 86.5 us -> 54.7 us
  matrix products: 44.4 us -> 69.3 us
  other arithmetic: 30 us -> 16.7 us
  starting transfers between devices: 17 us -> 26.1 us
    all_to_all x2 -> x0, waiting for transfers between devices: 163 us -> none  [the longest x1 96.5 us: shards(): lax.all_to_all(fields, 'gx', split_axis=2, concat_axis=1, tiled=True)]
    dot_general x1 -> x2, matrix products: 27.7 us -> 52.4 us  [the longest x1 46.7 us: line_derivative(): local = jnp.einsum('ij,fjyz->fiyz', near, source, precision=highest)]
    ppermute x0 -> x10, waiting for transfers between devices: none -> 24 us  [shifted_in(): lax.ppermute(array, axis, [(i, (i + shift) % peers) for i in range(peers)])]
    sub x1 -> x0, other arithmetic: 17.7 us -> none  [shards(): fields - advect * fields[0] * line_slope - advect * fields[2] * span_slope]
    ppermute x0 -> x10, starting transfers between devices: none -> 17.4 us  [shifted_in(): lax.ppermute(array, axis, [(i, (i + shift) % peers) for i in range(peers)])]
    all_to_all x2 -> x0, starting transfers between devices: 13.5 us -> none  [the longest x1 8.61 us: shards(): lax.all_to_all(fields, 'gx', split_axis=2, concat_axis=1, tiled=True)]
    all_to_all x3 -> x0, local copies, waits for them, and re-layouts: 9.87 us -> none  [the longest x2 6.56 us: shards(): lax.all_to_all(derivative, 'gx', split_axis=1, concat_axis=2, tiled=True)]
    slice x4 -> x1, local copies, waits for them, and re-layouts: 8.25 us -> 0.25 us  [line_derivative(): moments[:, 0]]
  transfers between devices with their start and end apart: 4 -> 14, of which waited for: 2 -> 6; matrix products, arithmetic and copies ran while one was open for 26% -> 28% of each run, Pallas kernels for 0% -> 0%
where the time goes in v1:
time: 236 us; the launch traced here: 232 us
  matrix products  69.3 us (29%)
  local copies, waits for them, and re-layouts  54.7 us (23%)
  blocking collectives  35.3 us (15%)
  starting transfers between devices  26.1 us (11%)
  waiting for transfers between devices  24 us (10%)
  other arithmetic  16.7 us (7%)
  loops' own time  4.7 us (2%)
    dot_general x1, matrix products, line_derivative(): local = jnp.einsum('ij,fjyz->fiyz', near, source, precision=highest)  46.7 us
    all_gather x2, blocking collectives, carried_in(): gathered = jax.tree.map(lambda a: lax.all_gather(a, axis), part)  24.8 us
    ppermute x10, waiting for transfers between devices, shifted_in(): lax.ppermute(array, axis, [(i, (i + shift) % peers) for i in range(peers)])  24 us
    unnamed x22, local copies, waits for them, and re-layouts  23.2 us
    ppermute x10, starting transfers between devices, shifted_in(): lax.ppermute(array, axis, [(i, (i + shift) % peers) for i in range(peers)])  17.4 us
    slice x2, local copies, waits for them, and re-layouts, extended(): leading = lax.slice_in_dim(array, 0, width, axis=dim)  10.9 us
    unnamed x1, blocking collectives  10.5 us
    dynamic_update_slice x256, local copies, waits for them, and re-layouts, wall_carries(): lax.scan(pivot_step, jnp.zeros_like(viscous), None, length=total_rows)  9.7 us
  transfers between devices with their start and end apart: 14, of which 6 were waited for; matrix products, arithmetic and copies ran while one was open for 28% of the time, Pallas kernels for 0%

profile of v1, /device:TPU:24, one launch (start us, length us, event | category | flops | bytes accessed | tf_op | source)
XLA Modules:
  0.0 232.0 jit_solution(11532148247964658109)
XLA Ops:
  0.0 1.1 fusion.103
  1.1 0.0 collective-permute-start.1
  1.1 5.3 %collective-permute-start = (f32[5,2,64,128]{3,2,1,0:T(8,128)S(1)}, f32[5,2,64,128]{3,2,1,0:T(8,128)S(1)}, u32[]{:S(2)}, u32[]{:S(2)}) collective-permute-start(f32[5,2,64,128]{3,2,1,0:T(8,128)S(1)} %get-tuple-element.251), channel_id=1, source_target_pairs={{16,0},{32,16},{48,32},{64,48},{80,64},{96,80},{112,96},{128,112},... | collective-permute-start | bytes 983048 | tf_op jit(solution)/shard_map/ppermute | solution.py:22
  6.5 9.8 %fusion.104 = (f32[5,32,64,3]{3,2,1,0:T(8,128)}, f32[5,32,64,3]{3,2,1,0:T(8,128)}) fusion(f32[5,32,64,128]{3,2,1,0:T(8,128)} %param.8), kind=kLoop, calls=%fused_computation.145 | loop fusion | bytes 491520 | tf_op jit(solution)/shard_map/slice | solution.py:20
  16.3 4.1 %copy.30 = f32[5,32,64,3]{2,1,3,0:T(8,128)} copy(f32[5,32,64,3]{3,2,1,0:T(8,128)} %get-tuple-element.257) | data formatting | bytes 245760
  20.4 0.7 collective-permute-start.12
  21.1 4.1 %copy.31 = f32[5,32,64,3]{2,1,3,0:T(8,128)} copy(f32[5,32,64,3]{3,2,1,0:T(8,128)} %get-tuple-element.258) | data formatting | bytes 245760
  25.2 2.6 %collective-permute-start.13 = (f32[5,32,64,3]{2,1,3,0:T(8,128)}, f32[5,32,64,3]{2,1,3,0:T(8,128)}, u32[]{:S(2)}, u32[]{:S(2)}) collective-permute-start(f32[5,32,64,3]{2,1,3,0:T(8,128)} %copy.31), channel_id=1, source_target_pairs={{0,1},{1,2},{2,3},{3,0},{4,5},{5,6},{6,7},{7,4},{8,9},{9,10},{10,1... | collective-permute-start | bytes 368648 | tf_op jit(solution)/shard_map/ppermute | solution.py:21
  27.9 18.1 %while.43 = (s32[]{:T(128)}, f32[5]{0:T(128)S(1)}, f32[256,5]{1,0:T(8,128)S(1)}, f32[5]{0:T(128)S(1)}, f32[5]{0:T(128)S(1)}, /*index=5*/s32[]{:T(128)}, s32[]{:T(128)}) while((s32[]{:T(128)}, f32[5]{0:T(128)S(1)}, f32[256,5]{1,0:T(8,128)S(1)}, f32[5]{0:T(128)S(1)}, f32[5]{0:T(128)S(1)}, /*index=5*/s32[]{:T(128)}, s32[]{:T(128)}) %tuple.81), condition=%wide.region_1.2_spmd.clone, body=%wide.region_0.1_spmd.clone.sunk | while | flops 23 | bytes 211 | solution.py:91
  46.0 0.1 copy.21
  46.0 0.1 multiply_log_fusion
  46.1 0.2 reduce_window_sum.11
  46.4 0.2 slice_reduce_fusion
  46.6 0.1 subtract_exponential_fusion
  46.7 1.8 multiply_bitcast_fusion.1
  48.5 4.0 %constant_dynamic-update-slice_fusion.1 = (f32[5,34,64,128]{3,2,1,0:T(8,128)S(1)}, f32[5,34,64,128]{3,2,1,0:T(8,128)S(1)}) fusion(f32[5,32,64,128]{3,2,1,0:T(8,128)} %param.8, f32[5,34,64,128]{3,2,1,0:T(8,128)S(1)} %constant_dynamic-update-slice_fusion.3), kind=kLoop, calls=%fused_computation.99 | loop fusion | bytes 15728640
  52.6 0.0 slice-start
  52.6 0.0 slice-start.1
  52.6 3.1 %fusion.17 = f32[5,32,64,128]{3,2,1,0:T(8,128)S(1)} fusion(f32[5,34,64,128]{3,2,1,0:T(8,128)S(1)} %get-tuple-element.254, f32[5,34,64,128]{3,2,1,0:T(8,128)S(1)} %constant_dynamic-update-slice_fusion), kind=kLoop, calls=%fused_computation.33 | loop fusion | flops 6553600 | bytes 26214400 | tf_op jit(solution)/shard_map/add | solution.py:143
  55.7 5.7 %fusion.40 = f32[5,2,64,128]{3,1,2,0:T(2,128)S(1)} fusion(f32[5,32,64,128]{3,2,1,0:T(8,128)S(1)} %fusion.17, f32[1,32]{1,0:T(1,128)S(1)} %get-tuple-element.264, f32[1,32]{1,0:T(1,128)S(1)} %get-tuple-element.265), kind=kOutput, calls=%fused_computation.53 | convolution fusion | flops 31457344 | bytes 5570816 | tf_op jit(solution)/shard_map/mj,fjyz->fmyz/dot_general | solution.py:148
  61.5 0.3 fusion.105
  61.7 0.0 collective-permute-start.2
  61.7 0.3 collective-permute-start.3
  62.1 0.0 copy-start.4
  62.1 5.4 %copy.13 = f32[5,32,64,128]{3,1,2,0:T(8,128)} copy(f32[5,32,64,128]{3,2,1,0:T(8,128)S(1)} %bitcast.70) | data formatting | bytes 10485760 | tf_op args[0]
  67.5 0.6 copy.12
  68.1 0.6 copy.20
  68.7 0.6 dynamic-slice
  70.0 0.2 dynamic-update-slice
  70.2 10.5 %all-reduce = f32[20]{0:T(128)S(1)} all-reduce(f32[20]{0:T(128)S(1)} %dynamic-update-slice), channel_id=2, replica_groups=mesh['gx'=16,'gy'=4,'gz'=4] {'gy'}, use_global_device_ids=true, to_apply=%add | all-reduce | flops 20 | bytes 160
  80.7 0.1 reshape.143
  80.8 4.4 %copy.16 = f32[5,32,64,3]{3,1,2,0:T(8,128)} copy(f32[5,32,64,3]{2,1,3,0:T(8,128)} %collective-permute-done.12) | data formatting | bytes 245760 | tf_op jit(solution)/shard_map/ppermute | solution.py:22
  85.2 4.4 %copy.18 = f32[5,32,64,3]{3,1,2,0:T(8,128)} copy(f32[5,32,64,3]{2,1,3,0:T(8,128)} %collective-permute-done.13) | data formatting | bytes 245760 | tf_op jit(solution)/shard_map/ppermute | solution.py:21
  89.6 0.8 collective-permute-start.7
  90.4 2.4 %collective-permute-start.8 = (f32[5,64,128]{2,1,0:T(8,128)S(1)}, f32[5,64,128]{2,1,0:T(8,128)S(1)}, u32[]{:S(2)}, u32[]{:S(2)}) collective-permute-start(f32[5,64,128]{2,1,0:T(8,128)S(1)} %bitcast.76), channel_id=1, source_target_pairs={{0,224},{16,240},{32,0},{48,16},{64,32},{80,48},{96,64},{112,80},{... | collective-permute-start | bytes 491528 | tf_op jit(solution)/shard_map/ppermute | solution.py:131
  92.8 1.0 multiply_add_fusion.8
  93.9 0.1 collective-permute-start.4
  94.0 3.0 %collective-permute-done.8 = f32[5,64,128]{2,1,0:T(8,128)S(1)} collective-permute-done((f32[5,64,128]{2,1,0:T(8,128)S(1)}, f32[5,64,128]{2,1,0:T(8,128)S(1)}, u32[]{:S(2)}, u32[]{:S(2)}) %collective-permute-start.8) | collective-permute-done | bytes 163872 | tf_op jit(solution)/shard_map/ppermute | solution.py:131
  97.0 3.8 %collective-permute-start.9 = (f32[5,64,128]{2,1,0:T(8,128)S(1)}, f32[5,64,128]{2,1,0:T(8,128)S(1)}, u32[]{:S(2)}, u32[]{:S(2)}) collective-permute-start(f32[5,64,128]{2,1,0:T(8,128)S(1)} %multiply_add_fusion.4), channel_id=1, source_target_pairs={{0,224},{16,240},{32,0},{48,16},{64,32},{80,48},{96,64},{112,80},{... | collective-permute-start | bytes 491528 | tf_op jit(solution)/shard_map/ppermute | solution.py:131
  100.8 0.7 collective-permute-done.4
  101.5 0.9 collective-permute-start.5
  102.4 1.6 collective-permute-done.9
  104.0 2.6 %collective-permute-start.10 = (f32[5,64,128]{2,1,0:T(8,128)S(1)}, f32[5,64,128]{2,1,0:T(8,128)S(1)}, u32[]{:S(2)}, u32[]{:S(2)}) collective-permute-start(f32[5,64,128]{2,1,0:T(8,128)S(1)} %multiply_add_fusion.3), channel_id=1, source_target_pairs={{0,192},{16,208},{32,224},{48,240},{64,0},{80,16},{96,32},{112,48}... | collective-permute-start | bytes 491528 | tf_op jit(solution)/shard_map/ppermute | solution.py:131
  106.6 4.9 %collective-permute-done.5 = f32[5,64,128]{2,1,0:T(8,128)S(1)} collective-permute-done((f32[5,64,128]{2,1,0:T(8,128)S(1)}, f32[5,64,128]{2,1,0:T(8,128)S(1)}, u32[]{:S(2)}, u32[]{:S(2)}) %collective-permute-start.5) | collective-permute-done | bytes 163872 | tf_op jit(solution)/shard_map/ppermute | solution.py:131
  111.6 4.6 %collective-permute-start.6 = (f32[5,64,128]{2,1,0:T(8,128)S(1)}, f32[5,64,128]{2,1,0:T(8,128)S(1)}, u32[]{:S(2)}, u32[]{:S(2)}) collective-permute-start(f32[5,64,128]{2,1,0:T(8,128)S(1)} %multiply_add_fusion.6), channel_id=1, source_target_pairs={{0,128},{16,144},{32,160},{48,176},{64,192},{80,208},{96,224},{112... | collective-permute-start | bytes 491528 | tf_op jit(solution)/shard_map/ppermute | solution.py:131
  116.2 1.9 collective-permute-start.11
  118.1 10.9 %collective-permute-done.6 = f32[5,64,128]{2,1,0:T(8,128)S(1)} collective-permute-done((f32[5,64,128]{2,1,0:T(8,128)S(1)}, f32[5,64,128]{2,1,0:T(8,128)S(1)}, u32[]{:S(2)}, u32[]{:S(2)}) %collective-permute-start.6) | collective-permute-done | bytes 163872 | tf_op jit(solution)/shard_map/ppermute | solution.py:131
  129.0 2.8 %collective-permute-done.11 = f32[5,64,128]{2,1,0:T(8,128)S(1)} collective-permute-done((f32[5,64,128]{2,1,0:T(8,128)S(1)}, f32[5,64,128]{2,1,0:T(8,128)S(1)}, u32[]{:S(2)}, u32[]{:S(2)}) %collective-permute-start.11) | collective-permute-done | bytes 163872 | tf_op jit(solution)/shard_map/ppermute | solution.py:131
  131.8 46.7 %fusion.9 = f32[5,32,64,128]{3,1,2,0:T(8,128)} fusion(f32[5,32,64,3]{3,1,2,0:T(8,128)} %copy.18, f32[5,32,64,128]{3,1,2,0:T(8,128)} %copy.13, f32[5,32,64,3]{3,1,2,0:T(8,128)} %copy.16, f32[32,64,128]{2,0,1:T(8,128)S(1)} %copy.20, f32[32,64,128]{2,0,1:T(8,128)S(1)} %copy.12, f32[5,64,128]{2,1,0:T(8,128)S(1)} %multiply_add_fusion.1, ...), kind=kOutput, calls=%fused_computation.22 | convolution fusion | flops 532164608 | bytes 18399488 | tf_op jit(solution)/shard_map/ij,fjyz->fiyz/dot_general | solution.py:149
  178.6 9.3 %fusion.35 = f32[5,32,64,128]{3,2,1,0:T(8,128)S(1)} fusion(f32[5,32,64,128]{3,1,2,0:T(8,128)} %fusion.9, f32[5,64]{1,0:T(8,128)S(1)} %reduce_window_sum.11, f32[5,64]{1,0:T(8,128)S(1)} %get-tuple-element.250, pred[64,64]{1,0:T(8,128)(4,1)S(1)} %iota_compare_fusion.1), kind=kOutput, calls=%fused_computation.52 | convolution fusion | flops 1006714880 | bytes 10492416 | tf_op jit(solution)/shard_map/fik,fxkz->fxiz/dot_general | solution.py:104
  187.8 0.0 copy-start.1
  187.9 2.3 %copy-done.1 = f32[5,32,64,128]{3,2,1,0:T(8,128)} copy-done((f32[5,32,64,128]{3,2,1,0:T(8,128)}, f32[5,32,64,128]{3,2,1,0:T(8,128)S(1)}, u32[]{:S(2)}) %copy-start.1) | copy-done | bytes 5242904
  190.2 0.1 slice.111
  190.3 12.4 %all-gather.1 = f32[20,32,1,128]{3,1,2,0:T(8,128)S(1)} all-gather(f32[5,32,1,128]{3,1,2,0:T(8,128)S(1)} %bitcast.73), channel_id=3, replica_groups=mesh['gx'=16,'gy'=4,'gz'=4] {'gy'}, dimensions={0}, use_global_device_ids=true | all-gather | bytes 409600 | tf_op jit(solution)/shard_map/all_gather | solution.py:31
  202.7 7.6 %fusion.32 = f32[5,32,64,128]{3,2,1,0:T(8,128)S(1)} fusion(f32[5,32,64,128]{3,2,1,0:T(8,128)} %copy-done.1, f32[5,32,128]{2,1,0:T(8,128)S(1)} %get-tuple-element.195, f32[5,64]{1,0:T(8,128)S(1)} %get-tuple-element.261, f32[5,64]{1,0:T(8,128)S(1)} %get-tuple-element.248, pred[64,64]{1,0:T(8,128)(4,1)S(1)} %iota_compare_fusion), kind=kOutput, calls=%fused_computation.51 | convolution fusion | flops 1009315840 | bytes 10574336 | tf_op jit(solution)/shard_map/fik,fxkz->fxiz/dot_general | solution.py:117
  210.3 0.0 copy-start
  210.3 2.3 %copy-done = f32[5,32,64,128]{3,2,1,0:T(8,128)} copy-done((f32[5,32,64,128]{3,2,1,0:T(8,128)}, f32[5,32,64,128]{3,2,1,0:T(8,128)S(1)}, u32[]{:S(2)}) %copy-start) | copy-done | bytes 5242904
  212.7 0.1 slice.112
  212.7 12.5 %all-gather.2 = f32[20,32,1,128]{3,1,2,0:T(8,128)S(1)} all-gather(f32[5,32,1,128]{3,1,2,0:T(8,128)S(1)} %bitcast.74), channel_id=4, replica_groups=mesh['gx'=16,'gy'=4,'gz'=4] {'gy'}, dimensions={0}, use_global_device_ids=true | all-gather | bytes 409600 | tf_op jit(solution)/shard_map/all_gather | solution.py:31
  225.2 0.4 while.42
  225.3 0.1 bitcast_add_fusion.6
  225.4 0.1 bitcast_add_fusion.6
  225.5 0.1 bitcast_add_fusion.6
  225.6 6.2 %multiply_add_fusion = f32[5,32,64,128]{3,2,1,0:T(8,128)} fusion(f32[5,32,64,128]{3,2,1,0:T(8,128)} %copy-done, f32[5,32,128]{2,1,0:T(8,128)S(1)} %get-tuple-element.196, f32[5,64]{1,0:T(8,128)S(1)} %get-tuple-element.247), kind=kLoop, calls=%fused_computation.41 | loop fusion | flops 2621440 | bytes 10568960 | tf_op jit(solution)/shard_map/add | solution.py:126
  (551 shorter events, 13.8 us)
Async XLA Ops:
  1.1 47.3 %collective-permute-start.1 = (f32[5,2,64,128]{3,2,1,0:T(8,128)S(1)}, f32[5,2,64,128]{3,2,1,0:T(8,128)S(1)}, u32[]{:S(2)}, u32[]{:S(2)}) collective-permute-start(f32[5,2,64,128]{3,2,1,0:T(8,128)S(1)} %get-tuple-element.252), channel_id=1, source_target_pairs={{0,16},{16,32},{32,48},{48,64},{64,80},{80,96},{96,112},{112,128},... | collective-permute-start | bytes 983048 | tf_op jit(solution)/shard_map/ppermute | solution.py:21
  1.1 51.4 %collective-permute-start = (f32[5,2,64,128]{3,2,1,0:T(8,128)S(1)}, f32[5,2,64,128]{3,2,1,0:T(8,128)S(1)}, u32[]{:S(2)}, u32[]{:S(2)}) collective-permute-start(f32[5,2,64,128]{3,2,1,0:T(8,128)S(1)} %get-tuple-element.251), channel_id=1, source_target_pairs={{16,0},{32,16},{48,32},{64,48},{80,64},{96,80},{112,96},{128,112},... | collective-permute-start | bytes 983048 | tf_op jit(solution)/shard_map/ppermute | solution.py:22
  16.3 11.6 %copy-start.3 = (f32[5]{0:T(128)S(1)}, f32[5]{0:T(128)}, u32[]{:S(2)}) copy-start(f32[5]{0:T(128)} %param.9) | copy-start | bytes 64
  20.4 60.4 %collective-permute-start.12 = (f32[5,32,64,3]{2,1,3,0:T(8,128)}, f32[5,32,64,3]{2,1,3,0:T(8,128)}, u32[]{:S(2)}, u32[]{:S(2)}) collective-permute-start(f32[5,32,64,3]{2,1,3,0:T(8,128)} %copy.30), channel_id=1, source_target_pairs={{1,0},{2,1},{3,2},{0,3},{5,4},{6,5},{7,6},{4,7},{9,8},{10,9},{11,1... | collective-permute-start | bytes 368648 | tf_op jit(solution)/shard_map/ppermute | solution.py:22
  25.2 60.0 %collective-permute-start.13 = (f32[5,32,64,3]{2,1,3,0:T(8,128)}, f32[5,32,64,3]{2,1,3,0:T(8,128)}, u32[]{:S(2)}, u32[]{:S(2)}) collective-permute-start(f32[5,32,64,3]{2,1,3,0:T(8,128)} %copy.31), channel_id=1, source_target_pairs={{0,1},{1,2},{2,3},{3,0},{4,5},{5,6},{6,7},{7,4},{8,9},{9,10},{10,1... | collective-permute-start | bytes 368648 | tf_op jit(solution)/shard_map/ppermute | solution.py:21
  52.6 9.5 %slice-start = ((s8[5242880]{0:T(1024)(128)(4,1)}), s8[4194304]{0:T(1024)(128)(4,1)S(1)}, s32[]{:S(2)}) async-start(s8[5242880]{0:T(1024)(128)(4,1)} %bitcast.69), calls=%async_computation | async-start | bytes 8388608
  52.6 9.5 %slice-start.1 = ((s8[5242880]{0:T(1024)(128)(4,1)}), s8[1048576]{0:T(1024)(128)(4,1)S(1)}, s32[]{:S(2)}) async-start(s8[5242880]{0:T(1024)(128)(4,1)} %bitcast.69), calls=%async_computation.1 | async-start | bytes 2097152
  55.7 11.8 %copy-start.2 = (f32[5,32,64,128]{3,2,1,0:T(8,128)}, f32[5,32,64,128]{3,2,1,0:T(8,128)S(1)}, u32[]{:S(2)}) copy-start(f32[5,32,64,128]{3,2,1,0:T(8,128)S(1)} %fusion.17) | copy-start | bytes 15728644
  61.7 31.1 %collective-permute-start.2 = (f32[5,64,128]{2,1,0:T(8,128)S(1)}, f32[5,64,128]{2,1,0:T(8,128)}, u32[]{:S(2)}, u32[]{:S(2)}) collective-permute-start(f32[5,64,128]{2,1,0:T(8,128)S(1)} %bitcast.77), channel_id=1, source_target_pairs={{0,16},{16,32},{32,48},{48,64},{64,80},{80,96},{96,112},{112,128},... | collective-permute-start | bytes 491528 | tf_op jit(solution)/shard_map/ppermute | solution.py:131
  61.7 31.1 %collective-permute-start.3 = (f32[5,64,128]{2,1,0:T(8,128)S(1)}, f32[5,64,128]{2,1,0:T(8,128)}, u32[]{:S(2)}, u32[]{:S(2)}) collective-permute-start(f32[5,64,128]{2,1,0:T(8,128)S(1)} %bitcast.78), channel_id=1, source_target_pairs={{0,32},{16,48},{32,64},{48,80},{64,96},{80,112},{96,128},{112,144}... | collective-permute-start | bytes 491528 | tf_op jit(solution)/shard_map/ppermute | solution.py:131
  62.1 6.6 %copy-start.4 = (u32[256]{0:T(256)S(1)}, u32[256]{0:T(256)}, u32[]{:S(2)}) copy-start(u32[256]{0:T(256)} %constant.140) | copy-start | bytes 3076
  89.6 4.3 %collective-permute-start.7 = (f32[5,64,128]{2,1,0:T(8,128)S(1)}, f32[5,64,128]{2,1,0:T(8,128)S(1)}, u32[]{:S(2)}, u32[]{:S(2)}) collective-permute-start(f32[5,64,128]{2,1,0:T(8,128)S(1)} %bitcast.75), channel_id=1, source_target_pairs={{0,240},{16,0},{32,16},{48,32},{64,48},{80,64},{96,80},{112,96},{1... | collective-permute-start | bytes 491528 | tf_op jit(solution)/shard_map/ppermute | solution.py:131
  90.4 6.5 %collective-permute-start.8 = (f32[5,64,128]{2,1,0:T(8,128)S(1)}, f32[5,64,128]{2,1,0:T(8,128)S(1)}, u32[]{:S(2)}, u32[]{:S(2)}) collective-permute-start(f32[5,64,128]{2,1,0:T(8,128)S(1)} %bitcast.76), channel_id=1, source_target_pairs={{0,224},{16,240},{32,0},{48,16},{64,32},{80,48},{96,64},{112,80},{... | collective-permute-start | bytes 491528 | tf_op jit(solution)/shard_map/ppermute | solution.py:131
  93.9 7.6 %collective-permute-start.4 = (f32[5,64,128]{2,1,0:T(8,128)S(1)}, f32[5,64,128]{2,1,0:T(8,128)S(1)}, u32[]{:S(2)}, u32[]{:S(2)}) collective-permute-start(f32[5,64,128]{2,1,0:T(8,128)S(1)} %multiply_add_fusion.8), channel_id=1, source_target_pairs={{0,32},{16,48},{32,64},{48,80},{64,96},{80,112},{96,128},{112,144}... | collective-permute-start | bytes 491528 | tf_op jit(solution)/shard_map/ppermute | solution.py:131
  97.0 7.0 %collective-permute-start.9 = (f32[5,64,128]{2,1,0:T(8,128)S(1)}, f32[5,64,128]{2,1,0:T(8,128)S(1)}, u32[]{:S(2)}, u32[]{:S(2)}) collective-permute-start(f32[5,64,128]{2,1,0:T(8,128)S(1)} %multiply_add_fusion.4), channel_id=1, source_target_pairs={{0,224},{16,240},{32,0},{48,16},{64,32},{80,48},{96,64},{112,80},{... | collective-permute-start | bytes 491528 | tf_op jit(solution)/shard_map/ppermute | solution.py:131
  101.5 10.0 %collective-permute-start.5 = (f32[5,64,128]{2,1,0:T(8,128)S(1)}, f32[5,64,128]{2,1,0:T(8,128)S(1)}, u32[]{:S(2)}, u32[]{:S(2)}) collective-permute-start(f32[5,64,128]{2,1,0:T(8,128)S(1)} %multiply_add_fusion.7), channel_id=1, source_target_pairs={{0,64},{16,80},{32,96},{48,112},{64,128},{80,144},{96,160},{112,17... | collective-permute-start | bytes 491528 | tf_op jit(solution)/shard_map/ppermute | solution.py:131
  104.0 12.1 %collective-permute-start.10 = (f32[5,64,128]{2,1,0:T(8,128)S(1)}, f32[5,64,128]{2,1,0:T(8,128)S(1)}, u32[]{:S(2)}, u32[]{:S(2)}) collective-permute-start(f32[5,64,128]{2,1,0:T(8,128)S(1)} %multiply_add_fusion.3), channel_id=1, source_target_pairs={{0,192},{16,208},{32,224},{48,240},{64,0},{80,16},{96,32},{112,48}... | collective-permute-start | bytes 491528 | tf_op jit(solution)/shard_map/ppermute | solution.py:131
  111.6 17.4 %collective-permute-start.6 = (f32[5,64,128]{2,1,0:T(8,128)S(1)}, f32[5,64,128]{2,1,0:T(8,128)S(1)}, u32[]{:S(2)}, u32[]{:S(2)}) collective-permute-start(f32[5,64,128]{2,1,0:T(8,128)S(1)} %multiply_add_fusion.6), channel_id=1, source_target_pairs={{0,128},{16,144},{32,160},{48,176},{64,192},{80,208},{96,224},{112... | collective-permute-start | bytes 491528 | tf_op jit(solution)/shard_map/ppermute | solution.py:131
  116.2 15.7 %collective-permute-start.11 = (f32[5,64,128]{2,1,0:T(8,128)S(1)}, f32[5,64,128]{2,1,0:T(8,128)S(1)}, u32[]{:S(2)}, u32[]{:S(2)}) collective-permute-start(f32[5,64,128]{2,1,0:T(8,128)S(1)} %multiply_add_fusion.2), channel_id=1, source_target_pairs={{0,128},{16,144},{32,160},{48,176},{64,192},{80,208},{96,224},{112... | collective-permute-start | bytes 491528 | tf_op jit(solution)/shard_map/ppermute | solution.py:131
  187.8 2.4 %copy-start.1 = (f32[5,32,64,128]{3,2,1,0:T(8,128)}, f32[5,32,64,128]{3,2,1,0:T(8,128)S(1)}, u32[]{:S(2)}) copy-start(f32[5,32,64,128]{3,2,1,0:T(8,128)S(1)} %fusion.35) | copy-start | bytes 15728644
  210.3 2.4 %copy-start = (f32[5,32,64,128]{3,2,1,0:T(8,128)}, f32[5,32,64,128]{3,2,1,0:T(8,128)S(1)}, u32[]{:S(2)}) copy-start(f32[5,32,64,128]{3,2,1,0:T(8,128)S(1)} %fusion.32) | copy-start | bytes 15728644

commit v2 on v1

v2 whole, which is shorter than its diff:
```python
import math

import jax
import jax.numpy as jnp
from jax import lax
from jax.experimental import pallas as pl
from jax.sharding import PartitionSpec as P

advect = 0.3
root_ratio = (-1.0 + math.sqrt(5.0) / 3.0) * 1.5
line_gain = (1.0 + root_ratio * root_ratio) / (1.0 - root_ratio * root_ratio)
highest = lax.Precision.HIGHEST


def extended(array, sides, width):
    for axis, dim in sides:
        peers, length = (lax.axis_size(axis), array.shape[dim])
        up = [(i, (i + 1) % peers) for i in range(peers)]
        down = [(j, i) for i, j in up]
        last = lax.slice_in_dim(array, length - width, length, axis=dim)
        leading = lax.slice_in_dim(array, 0, width, axis=dim)
        before = lax.ppermute(last, axis, up)
        after = lax.ppermute(leading, axis, down)
        array = jnp.concatenate([before, array, after], axis=dim)
    return array


def signed_power(exponent):
    parity = jnp.mod(exponent, 2.0)
    return (1.0 - 2.0 * parity) * jnp.exp(exponent * math.log(abs(root_ratio)))


def span_derivative(fields):
    padded = extended(fields, (("gz", 3),), 3)
    span_count = fields.shape[3]

    def shifted(offset):
        return padded[..., 3 + offset : 3 + offset + span_count]

    return (
        45.0 * (shifted(1) - shifted(-1))
        - 9.0 * (shifted(2) - shifted(-2))
        + (shifted(3) - shifted(-3))
    ) / 60.0


def wall_pivots(viscous, total_rows):
    root = jnp.sqrt(1.0 + 4.0 * viscous)
    upper = 0.5 * (1.0 + 2.0 * viscous + root)
    log_ratio = -2.0 * jnp.log1p((1.0 + root) / (2.0 * viscous))
    rows = jnp.arange(total_rows, dtype=jnp.float32)[None, :]
    ratio_rise = jnp.expm1((rows + 1.0) * log_ratio[:, None])
    ratio_next = jnp.expm1((rows + 2.0) * log_ratio[:, None])
    return ratio_rise / (ratio_next * upper[:, None])


def carried_over(line, gains, place, count, reverse):
    step = -1 if reverse else 1
    total = jnp.zeros_like(line)
    factor = jnp.ones_like(gains[0])
    for hop in range(1, count):
        pairs = [(i, i + step * hop) for i in range(count) if 0 <= i + step * hop < count]
        arrived = lax.ppermute(line, "gy", pairs)
        total = total + factor[:, None, None] * arrived
        between = jnp.clip(place - step * hop, 0, count - 1)
        factor = factor * lax.dynamic_index_in_dim(gains, between, 0, False)
    return total


def wall_carries(explicit, viscous):
    row_count = explicit.shape[2]
    count = lax.axis_size("gy")
    place = lax.axis_index("gy")
    total_rows = row_count * count
    all_pivots = wall_pivots(viscous, total_rows)
    all_log_gain = jnp.log(viscous[:, None] * all_pivots).reshape(viscous.shape[0], count, row_count)
    gains = jnp.exp(jnp.sum(all_log_gain, axis=2)).T
    pivots = lax.dynamic_index_in_dim(all_pivots.reshape(-1, count, row_count), place, 1, False)
    log_gain = lax.dynamic_index_in_dim(all_log_gain, place, 1, False)
    inclusive = jnp.cumsum(log_gain, axis=1)
    exclusive = inclusive - log_gain
    row_index = jnp.arange(row_count)[:, None]
    col_index = jnp.arange(row_count)[None, :]
    lower_mask = col_index <= row_index
    upper_mask = col_index >= row_index
    spread = inclusive[:, :, None] - inclusive[:, None, :]
    forward_table = jnp.where(
        lower_mask, pivots[:, None, :] * jnp.exp(jnp.where(lower_mask, spread, 0.0)), 0.0
    )
    eliminated_local = jnp.einsum("fik,fxkz->fxiz", forward_table, explicit, precision=highest)
    enter_low = carried_over(eliminated_local[:, :, -1], gains, place, count, False)
    eliminated = eliminated_local + jnp.exp(inclusive)[:, None, :, None] * enter_low[:, :, None, :]
    reach_log = exclusive[:, None, :] - exclusive[:, :, None]
    backward_table = jnp.where(upper_mask, jnp.exp(jnp.where(upper_mask, reach_log, 0.0)), 0.0)
    solved = jnp.einsum("fik,fxkz->fxiz", backward_table, eliminated, precision=highest)
    enter_high = carried_over(solved[:, :, 0], gains, place, count, True)
    trailing = jnp.exp(inclusive[:, -1:] - exclusive)
    return solved + trailing[:, None, :, None] * enter_high[:, :, None, :]


def shifted_in(array, axis, shift):
    peers = lax.axis_size(axis)
    return lax.ppermute(array, axis, [(i, (i + shift) % peers) for i in range(peers)])


def line_kernel(fields_ref, before_ref, after_ref, local_ref, moments_ref):
    length = fields_ref.shape[1]

    def plane(k):
        if k < 0:
            return before_ref[0, k + 2]
        if k >= length:
            return after_ref[0, k - length]
        return fields_ref[0, k]

    def source(i):
        return 7.0 / 9.0 * (plane(i + 1) - plane(i - 1)) + 1.0 / 36.0 * (plane(i + 2) - plane(i - 2))

    running = jnp.zeros(fields_ref.shape[2:], jnp.float32)
    for i in range(length):
        running = source(i) + root_ratio * running
        local_ref[0, i] = running
    moments_ref[0, 0] = running
    running = jnp.zeros(fields_ref.shape[2:], jnp.float32)
    for i in reversed(range(length)):
        value = source(i)
        running = value + root_ratio * running
        local_ref[0, i] = line_gain * (local_ref[0, i] + running - value)
    moments_ref[0, 1] = running


def line_local(fields, before, after):
    count, length, rows, cols = fields.shape
    block = lambda depth: pl.BlockSpec((1, depth, rows, cols), lambda f: (f, 0, 0, 0))
    size = fields.size * 4
    return pl.pallas_call(
        line_kernel,
        grid=(count,),
        in_specs=[block(length), block(2), block(2)],
        out_specs=[block(length), block(2)],
        out_shape=[
            jax.ShapeDtypeStruct(fields.shape, jnp.float32),
            jax.ShapeDtypeStruct((count, 2, rows, cols), jnp.float32),
        ],
        cost_estimate=pl.CostEstimate(flops=20 * fields.size, bytes_accessed=2 * size, transcendentals=0),
    )(fields, before, after)


def line_derivative(fields):
    peers = lax.axis_size("gx")
    length = fields.shape[1]
    total = length * peers
    before = shifted_in(fields[:, length - 2 :], "gx", 1)
    after = shifted_in(fields[:, :2], "gx", -1)
    local, moments = line_local(fields, before, after)
    index = jnp.arange(length, dtype=jnp.float32)
    block_weight = root_ratio**length
    left = shifted_in(moments[:, 0], "gx", 1) + block_weight * shifted_in(moments[:, 0], "gx", 2)
    right = shifted_in(moments[:, 1], "gx", -1) + block_weight * shifted_in(moments[:, 1], "gx", -2)
    span = 2
    while span < peers:
        weight = root_ratio ** (length * span)
        left = left + weight * shifted_in(left, "gx", span)
        right = right + weight * shifted_in(right, "gx", -span)
        span *= 2
    wrap = line_gain * root_ratio / (1.0 - root_ratio**total)
    rising = signed_power(index)[None, :, None, None]
    falling = signed_power(length - 1 - index)[None, :, None, None]
    return local + wrap * (rising * left[:, None] + falling * right[:, None])


def shards(fields, viscous):
    span_slope = span_derivative(fields)
    line_slope = line_derivative(fields)
    explicit = fields - advect * fields[0] * line_slope - advect * fields[2] * span_slope
    updated = wall_carries(explicit, viscous)
    return updated


def solution(mesh):
    in_specs = (P(None, "gx", "gy", "gz"), P())
    out_specs = P(None, "gx", "gy", "gz")
    return jax.shard_map(shards, mesh=mesh, in_specs=in_specs, out_specs=out_specs, check_vma=False)
```

time: 236 us -> 166 us (0.70); the launches traced: 232 us -> 166 us
  blocking collectives: 35.3 us -> 0 us
  matrix products: 69.3 us -> 40.9 us
  local copies, waits for them, and re-layouts: 54.7 us -> 32 us
  starting transfers between devices: 26.1 us -> 40.9 us
  waiting for transfers between devices: 24 us -> 37.8 us
  other arithmetic: 16.7 us -> 5.96 us
  Pallas kernels: 0 us -> 8.08 us
  loops' own time: 4.7 us -> 0 us
    dot_general x2 -> x0, matrix products: 52.4 us -> none  [the longest x1 46.7 us: line_derivative(): local = jnp.einsum('ij,fjyz->fiyz', near, source, precision=highest)]
    all_gather x2 -> x0, blocking collectives: 24.8 us -> none  [carried_in(): gathered = jax.tree.map(lambda a: lax.all_gather(a, axis), part)]
    dot_general x1, matrix products: 9.27 us -> 33.3 us  [wall_carries(): jnp.einsum('fik,fxkz->fxiz', forward_table, explicit, precision=highest)]
    unnamed x22 -> x8, local copies, waits for them, and re-layouts: 23.2 us -> 9.64 us
    ppermute x0 -> x6, starting transfers between devices: none -> 13.2 us  [carried_over(): arrived = lax.ppermute(line, 'gy', pairs)]
    unnamed x1 -> x0, blocking collectives: 10.5 us -> none
    ppermute x0 -> x6, waiting for transfers between devices: none -> 10.3 us  [carried_over(): arrived = lax.ppermute(line, 'gy', pairs)]
    dynamic_update_slice x256 -> x0, local copies, waits for them, and re-layouts: 9.7 us -> none  [wall_carries(): lax.scan(pivot_step, jnp.zeros_like(viscous), None, length=total_rows)]
  transfers between devices with their start and end apart: 14 -> 20, of which waited for: 6 -> 12; matrix products, arithmetic and copies ran while one was open for 28% -> 18% of each run, Pallas kernels for 0% -> 0%
where the time goes in v2:
time: 166 us
  starting transfers between devices  40.9 us (25%)
  matrix products  40.9 us (25%)
  waiting for transfers between devices  37.8 us (23%)
  local copies, waits for them, and re-layouts  32 us (19%)
  Pallas kernels  8.08 us (5%)
  other arithmetic  5.96 us (4%)
    dot_general x1, matrix products, wall_carries(): jnp.einsum('fik,fxkz->fxiz', forward_table, explicit, precision=highest)  33.3 us
    ppermute x12, waiting for transfers between devices, shifted_in(): lax.ppermute(array, axis, [(i, (i + shift) % peers) for i in range(peers)])  27.5 us
    ppermute x12, starting transfers between devices, shifted_in(): lax.ppermute(array, axis, [(i, (i + shift) % peers) for i in range(peers)])  24.4 us
    ppermute x6, starting transfers between devices, carried_over(): arrived = lax.ppermute(line, 'gy', pairs)  13.2 us
    ppermute x6, waiting for transfers between devices, carried_over(): arrived = lax.ppermute(line, 'gy', pairs)  10.3 us
    slice x1, local copies, waits for them, and re-layouts, extended(): leading = lax.slice_in_dim(array, 0, width, axis=dim)  9.73 us
    unnamed x8, local copies, waits for them, and re-layouts  9.64 us
    pallas_call x1, Pallas kernels, line_local(): pl.pallas_call(line_kernel, grid=(count,), in_specs=[block(length), block...  8.08 us
  transfers between devices with their start and end apart: 20, of which 12 were waited for; matrix products, arithmetic and copies ran while one was open for 18% of the time, Pallas kernels for 0%

profile of v2, /device:TPU:24, one launch (start us, length us, event | category | flops | bytes accessed | tf_op | source)
XLA Modules:
  0.0 165.9 jit_solution(14184952877249700184)
XLA Ops:
  0.0 1.1 fusion.93
  1.1 0.0 collective-permute-start
  1.1 5.3 %collective-permute-start.1 = (f32[5,2,64,128]{3,2,1,0:T(8,128)S(1)}, f32[5,2,64,128]{3,2,1,0:T(8,128)S(1)}, u32[]{:S(2)}, u32[]{:S(2)}) collective-permute-start(f32[5,2,64,128]{3,2,1,0:T(8,128)S(1)} %get-tuple-element.17), channel_id=1, source_target_pairs={{0,240},{16,0},{32,16},{48,32},{64,48},{80,64},{96,80},{112,96},{1... | collective-permute-start | bytes 983048 | tf_op jit(solution)/shard_map/ppermute | solution.py:103
  6.5 9.7 %fusion.94 = (f32[5,32,64,3]{3,2,1,0:T(8,128)}, f32[5,32,64,3]{3,2,1,0:T(8,128)}) fusion(f32[5,32,64,128]{3,2,1,0:T(8,128)} %fields_ref.1), kind=kLoop, calls=%fused_computation.130 | loop fusion | bytes 491520 | tf_op jit(solution)/shard_map/slice | solution.py:21
  16.2 4.1 %copy.12 = f32[5,32,64,3]{2,1,3,0:T(8,128)} copy(f32[5,32,64,3]{3,2,1,0:T(8,128)} %get-tuple-element.19) | data formatting | bytes 245760
  20.3 0.7 collective-permute-start.12
  21.0 4.1 %copy.13 = f32[5,32,64,3]{2,1,3,0:T(8,128)} copy(f32[5,32,64,3]{3,2,1,0:T(8,128)} %get-tuple-element.20) | data formatting | bytes 245760
  25.1 2.5 %collective-permute-start.13 = (f32[5,32,64,3]{2,1,3,0:T(8,128)}, f32[5,32,64,3]{2,1,3,0:T(8,128)}, u32[]{:S(2)}, u32[]{:S(2)}) collective-permute-start(f32[5,32,64,3]{2,1,3,0:T(8,128)} %copy.13), channel_id=1, source_target_pairs={{0,1},{1,2},{2,3},{3,0},{4,5},{5,6},{6,7},{7,4},{8,9},{9,10},{10,1... | collective-permute-start | bytes 368648 | tf_op jit(solution)/shard_map/ppermute | solution.py:22
  27.6 1.7 %multiply_bitcast_fusion.1 = (f32[32,64,128]{2,1,0:T(8,128)S(1)}, f32[32,64,128]{2,1,0:T(8,128)S(1)}) fusion(f32[5,32,64,128]{3,2,1,0:T(8,128)} %fields_ref.1), kind=kLoop, calls=%fused_computation.51 | loop fusion | flops 524288 | bytes 4194304 | tf_op jit(solution)/shard_map/mul | solution.py:175
  29.4 0.0 copy-done.2
  29.4 0.2 fusion.90
  29.6 0.2 reduce_window_sum.13
  29.8 0.2 slice_reduce_fusion
  30.0 0.1 subtract_exponential_fusion
  30.2 0.0 collective-permute-done.12
  30.2 4.1 %copy.7 = f32[5,32,64,3]{3,2,1,0:T(8,128)} copy(f32[5,32,64,3]{2,1,3,0:T(8,128)} %collective-permute-done.12) | data formatting | bytes 245760 | tf_op jit(solution)/shard_map/ppermute | solution.py:23
  34.3 0.0 collective-permute-done.13
  34.3 4.1 %copy.9 = f32[5,32,64,3]{3,2,1,0:T(8,128)} copy(f32[5,32,64,3]{2,1,3,0:T(8,128)} %collective-permute-done.13) | data formatting | bytes 245760 | tf_op jit(solution)/shard_map/ppermute | solution.py:22
  38.4 0.0 collective-permute-done.before_ref
  38.4 0.0 collective-permute-done.1.after_ref
  38.4 0.7 copy-done
  39.1 0.7 copy-done.1
  39.9 8.1 %shard_map.28 = (f32[5,32,64,128]{3,2,1,0:T(8,128)}, f32[5,2,64,128]{3,2,1,0:T(8,128)}) custom-call(f32[5,32,64,128]{3,2,1,0:T(8,128)} %fields_ref.1, f32[5,2,64,128]{3,2,1,0:T(8,128)} %copy-done, f32[5,2,64,128]{3,2,1,0:T(8,128)} %copy-done.1), custom_call_target="tpu_custom_call" | custom-call | flops 26214400 | bytes 10485760 | tf_op jit(solution)/shard_map/pallas_call | solution.py:136
  47.9 0.9 slice_bitcast_fusion
  48.9 0.0 collective-permute-start.2
  48.9 0.1 collective-permute-start.3
  49.0 0.9 slice_bitcast_fusion.1
  49.9 2.9 %collective-permute-start.7 = (f32[5,64,128]{2,1,0:T(8,128)S(1)}, f32[5,64,128]{2,1,0:T(8,128)S(1)}, u32[]{:S(2)}, u32[]{:S(2)}) collective-permute-start(f32[5,64,128]{2,1,0:T(8,128)S(1)} %slice_bitcast_fusion.1), channel_id=1, source_target_pairs={{0,240},{16,0},{32,16},{48,32},{64,48},{80,64},{96,80},{112,96},{1... | collective-permute-start | bytes 491528 | tf_op jit(solution)/shard_map/ppermute | solution.py:103
  52.8 1.7 %collective-permute-start.8 = (f32[5,64,128]{2,1,0:T(8,128)S(1)}, f32[5,64,128]{2,1,0:T(8,128)S(1)}, u32[]{:S(2)}, u32[]{:S(2)}) collective-permute-start(f32[5,64,128]{2,1,0:T(8,128)S(1)} %slice_bitcast_fusion.1), channel_id=1, source_target_pairs={{0,224},{16,240},{32,0},{48,16},{64,32},{80,48},{96,64},{112,80},{... | collective-permute-start | bytes 491528 | tf_op jit(solution)/shard_map/ppermute | solution.py:103
  54.5 1.4 collective-permute-done.2
  55.9 1.3 collective-permute-done.3
  57.3 0.1 collective-permute-start.4
  57.4 0.0 collective-permute-done.7
  57.4 1.7 collective-permute-done.8
  59.1 3.8 %collective-permute-start.9 = (f32[5,64,128]{2,1,0:T(8,128)S(1)}, f32[5,64,128]{2,1,0:T(8,128)S(1)}, u32[]{:S(2)}, u32[]{:S(2)}) collective-permute-start(f32[5,64,128]{2,1,0:T(8,128)S(1)} %multiply_add_fusion.4), channel_id=1, source_target_pairs={{0,224},{16,240},{32,0},{48,16},{64,32},{80,48},{96,64},{112,80},{... | collective-permute-start | bytes 491528 | tf_op jit(solution)/shard_map/ppermute | solution.py:103
  62.8 2.8 %collective-permute-done.4 = f32[5,64,128]{2,1,0:T(8,128)S(1)} collective-permute-done((f32[5,64,128]{2,1,0:T(8,128)S(1)}, f32[5,64,128]{2,1,0:T(8,128)S(1)}, u32[]{:S(2)}, u32[]{:S(2)}) %collective-permute-start.4) | collective-permute-done | bytes 163872 | tf_op jit(solution)/shard_map/ppermute | solution.py:103
  65.6 0.1 collective-permute-start.5
  65.7 0.0 collective-permute-done.9
  65.7 4.2 %collective-permute-start.10 = (f32[5,64,128]{2,1,0:T(8,128)S(1)}, f32[5,64,128]{2,1,0:T(8,128)S(1)}, u32[]{:S(2)}, u32[]{:S(2)}) collective-permute-start(f32[5,64,128]{2,1,0:T(8,128)S(1)} %multiply_add_fusion.3), channel_id=1, source_target_pairs={{0,192},{16,208},{32,224},{48,240},{64,0},{80,16},{96,32},{112,48}... | collective-permute-start | bytes 491528 | tf_op jit(solution)/shard_map/ppermute | solution.py:103
  69.9 6.0 %collective-permute-done.5 = f32[5,64,128]{2,1,0:T(8,128)S(1)} collective-permute-done((f32[5,64,128]{2,1,0:T(8,128)S(1)}, f32[5,64,128]{2,1,0:T(8,128)S(1)}, u32[]{:S(2)}, u32[]{:S(2)}) %collective-permute-start.5) | collective-permute-done | bytes 163872 | tf_op jit(solution)/shard_map/ppermute | solution.py:103
  75.9 4.4 %collective-permute-start.6 = (f32[5,64,128]{2,1,0:T(8,128)S(1)}, f32[5,64,128]{2,1,0:T(8,128)S(1)}, u32[]{:S(2)}, u32[]{:S(2)}) collective-permute-start(f32[5,64,128]{2,1,0:T(8,128)S(1)} %multiply_add_fusion.6), channel_id=1, source_target_pairs={{0,128},{16,144},{32,160},{48,176},{64,192},{80,208},{96,224},{112... | collective-permute-start | bytes 491528 | tf_op jit(solution)/shard_map/ppermute | solution.py:103
  80.3 0.0 collective-permute-done.10
  80.3 1.9 %collective-permute-start.11 = (f32[5,64,128]{2,1,0:T(8,128)S(1)}, f32[5,64,128]{2,1,0:T(8,128)S(1)}, u32[]{:S(2)}, u32[]{:S(2)}) collective-permute-start(f32[5,64,128]{2,1,0:T(8,128)S(1)} %multiply_add_fusion.2), channel_id=1, source_target_pairs={{0,128},{16,144},{32,160},{48,176},{64,192},{80,208},{96,224},{112... | collective-permute-start | bytes 491528 | tf_op jit(solution)/shard_map/ppermute | solution.py:103
  82.2 10.8 %collective-permute-done.6 = f32[5,64,128]{2,1,0:T(8,128)S(1)} collective-permute-done((f32[5,64,128]{2,1,0:T(8,128)S(1)}, f32[5,64,128]{2,1,0:T(8,128)S(1)}, u32[]{:S(2)}, u32[]{:S(2)}) %collective-permute-start.6) | collective-permute-done | bytes 163872 | tf_op jit(solution)/shard_map/ppermute | solution.py:103
  93.1 3.6 %collective-permute-done.11 = f32[5,64,128]{2,1,0:T(8,128)S(1)} collective-permute-done((f32[5,64,128]{2,1,0:T(8,128)S(1)}, f32[5,64,128]{2,1,0:T(8,128)S(1)}, u32[]{:S(2)}, u32[]{:S(2)}) %collective-permute-start.11) | collective-permute-done | bytes 163872 | tf_op jit(solution)/shard_map/ppermute | solution.py:103
  96.6 33.3 %fusion.45 = f32[5,32,64,128]{3,2,1,0:T(8,128)} fusion(f32[5,32,64,3]{3,2,1,0:T(8,128)} %copy.9, f32[5,32,64,128]{3,2,1,0:T(8,128)} %fields_ref.1, f32[5,32,64,3]{3,2,1,0:T(8,128)} %copy.7, f32[5,32,64,128]{3,2,1,0:T(8,128)} %get-tuple-element.7, f32[32,64,128]{2,1,0:T(8,128)S(1)} %get-tuple-element.16, f32[5,64,128]{2,1,0:T(8,128)S(1)} %multiply_add_fusion.1, ...), kind=kOutput, calls=%fused_computation.49 | convolution fusion | flops 1035550720 | bytes 18420736 | tf_op jit(solution)/shard_map/fik,fxkz->fxiz/dot_general | solution.py:90
  130.0 1.2 slice.85
  131.2 3.4 %collective-permute-start.14 = (f32[5,32,128]{2,1,0:T(8,128)S(1)}, f32[5,32,128]{2,1,0:T(8,128)S(1)}, u32[]{:S(2)}, u32[]{:S(2)}) collective-permute-start(f32[5,32,128]{2,1,0:T(8,128)S(1)} %bitcast.50), channel_id=1, source_target_pairs={{0,4},{4,8},{8,12},{1,5},{5,9},{9,13},{2,6},{6,10},{10,14},{3,7},{... | collective-permute-start | bytes 245768 | tf_op jit(solution)/shard_map/ppermute | solution.py:63
  134.6 4.6 %collective-permute-start.15 = (f32[5,32,128]{2,1,0:T(8,128)S(1)}, f32[5,32,128]{2,1,0:T(8,128)S(1)}, u32[]{:S(2)}, u32[]{:S(2)}) collective-permute-start(f32[5,32,128]{2,1,0:T(8,128)S(1)} %bitcast.51), channel_id=1, source_target_pairs={{0,8},{4,12},{1,9},{5,13},{2,10},{6,14},{3,11},{7,15},{16,24},{20,... | collective-permute-start | bytes 245768 | tf_op jit(solution)/shard_map/ppermute | solution.py:63
  139.2 1.3 collective-permute-start.16
  140.5 0.0 collective-permute-done.14
  140.6 0.7 collective-permute-done.15
  141.3 1.3 collective-permute-done.16
  142.6 0.1 multiply_add_fusion.10
  142.6 7.6 %fusion.42 = f32[5,32,64,128]{3,2,1,0:T(8,128)S(1)} fusion(f32[5,32,64,128]{3,2,1,0:T(8,128)} %fusion.45, f32[5,32,128]{2,1,0:T(8,128)S(1)} %multiply_add_fusion.10, f32[5,64]{1,0:T(8,128)S(1)} %get-tuple-element.24, f32[5,64]{1,0:T(8,128)S(1)} %get-tuple-element.10, f32[5,64]{1,0:T(8,128)S(1)} %fusion.68, pred[64,64]{1,0:T(8,128)(4,1)S(1)} %iota_compare_fusion), kind=kOutput, calls=%fused_computation.48 | convolution fusion | flops 1009315840 | bytes 10575616 | tf_op jit(solution)/shard_map/fik,fxkz->fxiz/dot_general | solution.py:95
  150.2 0.1 slice.86
  150.3 1.3 collective-permute-start.17
  151.6 1.3 collective-permute-start.18
  152.9 1.3 collective-permute-start.19
  154.2 2.4 %collective-permute-done.17 = f32[5,32,128]{2,1,0:T(8,128)S(1)} collective-permute-done((f32[5,32,128]{2,1,0:T(8,128)S(1)}, f32[5,32,128]{2,1,0:T(8,128)S(1)}, u32[]{:S(2)}, u32[]{:S(2)}) %collective-permute-start.17) | collective-permute-done | bytes 81952 | tf_op jit(solution)/shard_map/ppermute | solution.py:63
  156.7 2.9 %collective-permute-done.18 = f32[5,32,128]{2,1,0:T(8,128)S(1)} collective-permute-done((f32[5,32,128]{2,1,0:T(8,128)S(1)}, f32[5,32,128]{2,1,0:T(8,128)S(1)}, u32[]{:S(2)}, u32[]{:S(2)}) %collective-permute-start.18) | collective-permute-done | bytes 81952 | tf_op jit(solution)/shard_map/ppermute | solution.py:63
  159.6 3.0 %collective-permute-done.19 = f32[5,32,128]{2,1,0:T(8,128)S(1)} collective-permute-done((f32[5,32,128]{2,1,0:T(8,128)S(1)}, f32[5,32,128]{2,1,0:T(8,128)S(1)}, u32[]{:S(2)}, u32[]{:S(2)}) %collective-permute-start.19) | collective-permute-done | bytes 81952 | tf_op jit(solution)/shard_map/ppermute | solution.py:63
  162.6 0.1 multiply_add_fusion.9
  162.6 3.3 %multiply_add_fusion = f32[5,32,64,128]{3,2,1,0:T(8,128)} fusion(f32[5,32,64,128]{3,2,1,0:T(8,128)S(1)} %fusion.42, f32[5,32,128]{2,1,0:T(8,128)S(1)} %multiply_add_fusion.9, f32[5,64]{1,0:T(8,128)S(1)} %get-tuple-element.9), kind=kLoop, calls=%fused_computation.26 | loop fusion | flops 2621440 | bytes 10568960 | tf_op jit(solution)/shard_map/add | solution.py:98
  (21 shorter events, 0.3 us)
Async XLA Ops:
  1.1 37.3 %collective-permute-start = (f32[5,2,64,128]{3,2,1,0:T(8,128)S(1)}, f32[5,2,64,128]{3,2,1,0:T(8,128)S(1)}, u32[]{:S(2)}, u32[]{:S(2)}) collective-permute-start(f32[5,2,64,128]{3,2,1,0:T(8,128)S(1)} %get-tuple-element.18), channel_id=1, source_target_pairs={{0,16},{16,32},{32,48},{48,64},{64,80},{80,96},{96,112},{112,128},... | collective-permute-start | bytes 983048 | tf_op jit(solution)/shard_map/ppermute | solution.py:103
  1.1 37.3 %collective-permute-start.1 = (f32[5,2,64,128]{3,2,1,0:T(8,128)S(1)}, f32[5,2,64,128]{3,2,1,0:T(8,128)S(1)}, u32[]{:S(2)}, u32[]{:S(2)}) collective-permute-start(f32[5,2,64,128]{3,2,1,0:T(8,128)S(1)} %get-tuple-element.17), channel_id=1, source_target_pairs={{0,240},{16,0},{32,16},{48,32},{64,48},{80,64},{96,80},{112,96},{1... | collective-permute-start | bytes 983048 | tf_op jit(solution)/shard_map/ppermute | solution.py:103
  20.3 9.1 %copy-start.2 = (f32[5]{0:T(128)S(1)}, f32[5]{0:T(128)}, u32[]{:S(2)}) copy-start(f32[5]{0:T(128)} %param.3) | copy-start | bytes 64
  20.3 9.9 %collective-permute-start.12 = (f32[5,32,64,3]{2,1,3,0:T(8,128)}, f32[5,32,64,3]{2,1,3,0:T(8,128)}, u32[]{:S(2)}, u32[]{:S(2)}) collective-permute-start(f32[5,32,64,3]{2,1,3,0:T(8,128)} %copy.12), channel_id=1, source_target_pairs={{1,0},{2,1},{3,2},{0,3},{5,4},{6,5},{7,6},{4,7},{9,8},{10,9},{11,1... | collective-permute-start | bytes 368648 | tf_op jit(solution)/shard_map/ppermute | solution.py:23
  25.1 9.2 %collective-permute-start.13 = (f32[5,32,64,3]{2,1,3,0:T(8,128)}, f32[5,32,64,3]{2,1,3,0:T(8,128)}, u32[]{:S(2)}, u32[]{:S(2)}) collective-permute-start(f32[5,32,64,3]{2,1,3,0:T(8,128)} %copy.13), channel_id=1, source_target_pairs={{0,1},{1,2},{2,3},{3,0},{4,5},{5,6},{6,7},{7,4},{8,9},{9,10},{10,1... | collective-permute-start | bytes 368648 | tf_op jit(solution)/shard_map/ppermute | solution.py:22
  38.4 0.7 copy-start
  39.1 0.7 copy-start.1
  48.9 7.1 %collective-permute-start.2 = (f32[5,64,128]{2,1,0:T(8,128)S(1)}, f32[5,64,128]{2,1,0:T(8,128)S(1)}, u32[]{:S(2)}, u32[]{:S(2)}) collective-permute-start(f32[5,64,128]{2,1,0:T(8,128)S(1)} %slice_bitcast_fusion), channel_id=1, source_target_pairs={{0,16},{16,32},{32,48},{48,64},{64,80},{80,96},{96,112},{112,128},... | collective-permute-start | bytes 491528 | tf_op jit(solution)/shard_map/ppermute | solution.py:103
  48.9 8.4 %collective-permute-start.3 = (f32[5,64,128]{2,1,0:T(8,128)S(1)}, f32[5,64,128]{2,1,0:T(8,128)S(1)}, u32[]{:S(2)}, u32[]{:S(2)}) collective-permute-start(f32[5,64,128]{2,1,0:T(8,128)S(1)} %slice_bitcast_fusion), channel_id=1, source_target_pairs={{0,32},{16,48},{32,64},{48,80},{64,96},{80,112},{96,128},{112,144}... | collective-permute-start | bytes 491528 | tf_op jit(solution)/shard_map/ppermute | solution.py:103
  49.9 7.5 %collective-permute-start.7 = (f32[5,64,128]{2,1,0:T(8,128)S(1)}, f32[5,64,128]{2,1,0:T(8,128)S(1)}, u32[]{:S(2)}, u32[]{:S(2)}) collective-permute-start(f32[5,64,128]{2,1,0:T(8,128)S(1)} %slice_bitcast_fusion.1), channel_id=1, source_target_pairs={{0,240},{16,0},{32,16},{48,32},{64,48},{80,64},{96,80},{112,96},{1... | collective-permute-start | bytes 491528 | tf_op jit(solution)/shard_map/ppermute | solution.py:103
  52.8 6.3 %collective-permute-start.8 = (f32[5,64,128]{2,1,0:T(8,128)S(1)}, f32[5,64,128]{2,1,0:T(8,128)S(1)}, u32[]{:S(2)}, u32[]{:S(2)}) collective-permute-start(f32[5,64,128]{2,1,0:T(8,128)S(1)} %slice_bitcast_fusion.1), channel_id=1, source_target_pairs={{0,224},{16,240},{32,0},{48,16},{64,32},{80,48},{96,64},{112,80},{... | collective-permute-start | bytes 491528 | tf_op jit(solution)/shard_map/ppermute | solution.py:103
  57.3 8.3 %collective-permute-start.4 = (f32[5,64,128]{2,1,0:T(8,128)S(1)}, f32[5,64,128]{2,1,0:T(8,128)S(1)}, u32[]{:S(2)}, u32[]{:S(2)}) collective-permute-start(f32[5,64,128]{2,1,0:T(8,128)S(1)} %multiply_add_fusion.8), channel_id=1, source_target_pairs={{0,32},{16,48},{32,64},{48,80},{64,96},{80,112},{96,128},{112,144}... | collective-permute-start | bytes 491528 | tf_op jit(solution)/shard_map/ppermute | solution.py:103
  59.1 6.6 %collective-permute-start.9 = (f32[5,64,128]{2,1,0:T(8,128)S(1)}, f32[5,64,128]{2,1,0:T(8,128)S(1)}, u32[]{:S(2)}, u32[]{:S(2)}) collective-permute-start(f32[5,64,128]{2,1,0:T(8,128)S(1)} %multiply_add_fusion.4), channel_id=1, source_target_pairs={{0,224},{16,240},{32,0},{48,16},{64,32},{80,48},{96,64},{112,80},{... | collective-permute-start | bytes 491528 | tf_op jit(solution)/shard_map/ppermute | solution.py:103
  65.6 10.3 %collective-permute-start.5 = (f32[5,64,128]{2,1,0:T(8,128)S(1)}, f32[5,64,128]{2,1,0:T(8,128)S(1)}, u32[]{:S(2)}, u32[]{:S(2)}) collective-permute-start(f32[5,64,128]{2,1,0:T(8,128)S(1)} %multiply_add_fusion.7), channel_id=1, source_target_pairs={{0,64},{16,80},{32,96},{48,112},{64,128},{80,144},{96,160},{112,17... | collective-permute-start | bytes 491528 | tf_op jit(solution)/shard_map/ppermute | solution.py:103
  65.7 14.5 %collective-permute-start.10 = (f32[5,64,128]{2,1,0:T(8,128)S(1)}, f32[5,64,128]{2,1,0:T(8,128)S(1)}, u32[]{:S(2)}, u32[]{:S(2)}) collective-permute-start(f32[5,64,128]{2,1,0:T(8,128)S(1)} %multiply_add_fusion.3), channel_id=1, source_target_pairs={{0,192},{16,208},{32,224},{48,240},{64,0},{80,16},{96,32},{112,48}... | collective-permute-start | bytes 491528 | tf_op jit(solution)/shard_map/ppermute | solution.py:103
  75.9 17.1 %collective-permute-start.6 = (f32[5,64,128]{2,1,0:T(8,128)S(1)}, f32[5,64,128]{2,1,0:T(8,128)S(1)}, u32[]{:S(2)}, u32[]{:S(2)}) collective-permute-start(f32[5,64,128]{2,1,0:T(8,128)S(1)} %multiply_add_fusion.6), channel_id=1, source_target_pairs={{0,128},{16,144},{32,160},{48,176},{64,192},{80,208},{96,224},{112... | collective-permute-start | bytes 491528 | tf_op jit(solution)/shard_map/ppermute | solution.py:103
  80.3 16.3 %collective-permute-start.11 = (f32[5,64,128]{2,1,0:T(8,128)S(1)}, f32[5,64,128]{2,1,0:T(8,128)S(1)}, u32[]{:S(2)}, u32[]{:S(2)}) collective-permute-start(f32[5,64,128]{2,1,0:T(8,128)S(1)} %multiply_add_fusion.2), channel_id=1, source_target_pairs={{0,128},{16,144},{32,160},{48,176},{64,192},{80,208},{96,224},{112... | collective-permute-start | bytes 491528 | tf_op jit(solution)/shard_map/ppermute | solution.py:103
  131.2 9.4 %collective-permute-start.14 = (f32[5,32,128]{2,1,0:T(8,128)S(1)}, f32[5,32,128]{2,1,0:T(8,128)S(1)}, u32[]{:S(2)}, u32[]{:S(2)}) collective-permute-start(f32[5,32,128]{2,1,0:T(8,128)S(1)} %bitcast.50), channel_id=1, source_target_pairs={{0,4},{4,8},{8,12},{1,5},{5,9},{9,13},{2,6},{6,10},{10,14},{3,7},{... | collective-permute-start | bytes 245768 | tf_op jit(solution)/shard_map/ppermute | solution.py:63
  134.6 6.7 %collective-permute-start.15 = (f32[5,32,128]{2,1,0:T(8,128)S(1)}, f32[5,32,128]{2,1,0:T(8,128)S(1)}, u32[]{:S(2)}, u32[]{:S(2)}) collective-permute-start(f32[5,32,128]{2,1,0:T(8,128)S(1)} %bitcast.51), channel_id=1, source_target_pairs={{0,8},{4,12},{1,9},{5,13},{2,10},{6,14},{3,11},{7,15},{16,24},{20,... | collective-permute-start | bytes 245768 | tf_op jit(solution)/shard_map/ppermute | solution.py:63
  139.2 3.3 %collective-permute-start.16 = (f32[5,32,128]{2,1,0:T(8,128)S(1)}, f32[5,32,128]{2,1,0:T(8,128)S(1)}, u32[]{:S(2)}, u32[]{:S(2)}) collective-permute-start(f32[5,32,128]{2,1,0:T(8,128)S(1)} %bitcast.52), channel_id=1, source_target_pairs={{0,12},{1,13},{2,14},{3,15},{16,28},{17,29},{18,30},{19,31},{32,44... | collective-permute-start | bytes 245768 | tf_op jit(solution)/shard_map/ppermute | solution.py:63
  150.3 6.3 %collective-permute-start.17 = (f32[5,32,128]{2,1,0:T(8,128)S(1)}, f32[5,32,128]{2,1,0:T(8,128)S(1)}, u32[]{:S(2)}, u32[]{:S(2)}) collective-permute-start(f32[5,32,128]{2,1,0:T(8,128)S(1)} %bitcast.53), channel_id=1, source_target_pairs={{4,0},{8,4},{12,8},{5,1},{9,5},{13,9},{6,2},{10,6},{14,10},{7,3},{... | collective-permute-start | bytes 245768 | tf_op jit(solution)/shard_map/ppermute | solution.py:63
  151.6 7.9 %collective-permute-start.18 = (f32[5,32,128]{2,1,0:T(8,128)S(1)}, f32[5,32,128]{2,1,0:T(8,128)S(1)}, u32[]{:S(2)}, u32[]{:S(2)}) collective-permute-start(f32[5,32,128]{2,1,0:T(8,128)S(1)} %bitcast.54), channel_id=1, source_target_pairs={{8,0},{12,4},{9,1},{13,5},{10,2},{14,6},{11,3},{15,7},{24,16},{28,... | collective-permute-start | bytes 245768 | tf_op jit(solution)/shard_map/ppermute | solution.py:63
  152.9 9.6 %collective-permute-start.19 = (f32[5,32,128]{2,1,0:T(8,128)S(1)}, f32[5,32,128]{2,1,0:T(8,128)S(1)}, u32[]{:S(2)}, u32[]{:S(2)}) collective-permute-start(f32[5,32,128]{2,1,0:T(8,128)S(1)} %bitcast.55), channel_id=1, source_target_pairs={{12,0},{13,1},{14,2},{15,3},{28,16},{29,17},{30,18},{31,19},{44,32... | collective-permute-start | bytes 245768 | tf_op jit(solution)/shard_map/ppermute | solution.py:63

commit v3 on v2

--- a/solution.py
+++ b/solution.py
@@ -146,14 +146,8 @@
     )(fields, before, after)
 
 
-def line_derivative(fields):
+def line_carries(moments, length):
     peers = lax.axis_size("gx")
-    length = fields.shape[1]
-    total = length * peers
-    before = shifted_in(fields[:, length - 2 :], "gx", 1)
-    after = shifted_in(fields[:, :2], "gx", -1)
-    local, moments = line_local(fields, before, after)
-    index = jnp.arange(length, dtype=jnp.float32)
     block_weight = root_ratio**length
     left = shifted_in(moments[:, 0], "gx", 1) + block_weight * shifted_in(moments[:, 0], "gx", 2)
     right = shifted_in(moments[:, 1], "gx", -1) + block_weight * shifted_in(moments[:, 1], "gx", -2)
@@ -163,16 +157,26 @@
         left = left + weight * shifted_in(left, "gx", span)
         right = right + weight * shifted_in(right, "gx", -span)
         span *= 2
+    return left, right
+
+
+def shards(fields, viscous):
+    length = fields.shape[1]
+    total = length * lax.axis_size("gx")
+    before = shifted_in(fields[:, length - 2 :], "gx", 1)
+    after = shifted_in(fields[:, :2], "gx", -1)
+    local, moments = line_local(fields, before, after)
+    late_fields, local = lax.optimization_barrier((fields, local))
+    span_slope = span_derivative(late_fields)
+    partial = late_fields - advect * late_fields[0] * local - advect * late_fields[2] * span_slope
+    left, right = line_carries(moments, length)
+    partial, left, right = lax.optimization_barrier((partial, left, right))
+    index = jnp.arange(length, dtype=jnp.float32)
     wrap = line_gain * root_ratio / (1.0 - root_ratio**total)
     rising = signed_power(index)[None, :, None, None]
     falling = signed_power(length - 1 - index)[None, :, None, None]
-    return local + wrap * (rising * left[:, None] + falling * right[:, None])
-
-
-def shards(fields, viscous):
-    span_slope = span_derivative(fields)
-    line_slope = line_derivative(fields)
-    explicit = fields - advect * fields[0] * line_slope - advect * fields[2] * span_slope
+    carried = wrap * (rising * left[:, None] + falling * right[:, None])
+    explicit = partial - advect * fields[0] * carried
     updated = wall_carries(explicit, viscous)
     return updated
 

time: 166 us -> 172 us (1.036)
  the two profiles are of different devices: /device:TPU:24 before, /device:TPU:32 now
where the time goes in v3:
time: 172 us
  waiting for transfers between devices  44.3 us (26%)
  other arithmetic  42.9 us (25%)
  starting transfers between devices  37.1 us (22%)
  local copies, waits for them, and re-layouts  26.8 us (16%)
  matrix products  12.2 us (7%)
  Pallas kernels  8.07 us (5%)
    ppermute x12, waiting for transfers between devices, shifted_in(): lax.ppermute(array, axis, [(i, (i + shift) % peers) for i in range(peers)])  29.4 us
    sub x1, other arithmetic, shards(): late_fields - advect * late_fields[0] * local  29.3 us
    ppermute x12, starting transfers between devices, shifted_in(): lax.ppermute(array, axis, [(i, (i + shift) % peers) for i in range(peers)])  20.6 us
    ppermute x6, starting transfers between devices, carried_over(): arrived = lax.ppermute(line, 'gy', pairs)  13.4 us
    optimization_barrier x1, local copies, waits for them, and re-layouts, shards(): late_fields, local = lax.optimization_barrier((fields, local))  11.1 us
    ppermute x6, waiting for transfers between devices, carried_over(): arrived = lax.ppermute(line, 'gy', pairs)  10.1 us
    pallas_call x1, Pallas kernels, line_local(): pl.pallas_call(line_kernel, grid=(count,), in_specs=[block(length), block...  8.07 us
    dot_general x1, matrix products, wall_carries(): jnp.einsum('fik,fxkz->fxiz', forward_table, explicit, precision=highest)  6.29 us
  transfers between devices with their start and end apart: 20, of which 10 were waited for; matrix products, arithmetic and copies ran while one was open for 36% of the time, Pallas kernels for 0%

profile of v3, /device:TPU:32, one launch (start us, length us, event | category | flops | bytes accessed | tf_op | source)
XLA Modules:
  0.0 171.6 jit_solution(10510469556273362315)
XLA Ops:
  0.0 1.1 fusion.77
  1.1 0.0 collective-permute-start
  1.1 1.7 %collective-permute-start.1 = (f32[5,2,64,128]{3,2,1,0:T(8,128)S(1)}, f32[5,2,64,128]{3,2,1,0:T(8,128)S(1)}, u32[]{:S(2)}, u32[]{:S(2)}) collective-permute-start(f32[5,2,64,128]{3,2,1,0:T(8,128)S(1)} %get-tuple-element.29), channel_id=1, source_target_pairs={{0,240},{16,0},{32,16},{48,32},{64,48},{80,64},{96,80},{112,96},{1... | collective-permute-start | bytes 983048 | tf_op jit(solution)/shard_map/ppermute | solution.py:103
  2.9 0.6 iota_compare_fusion.1
  3.5 0.7 log-plus-one_multiply_fusion
  4.2 0.8 fusion.73
  5.0 0.6 dynamic-slice_bitcast_fusion
  5.6 0.2 reduce_window_sum.13
  5.8 0.2 slice_reduce_fusion
  6.0 0.6 fusion.55
  6.6 0.6 iota_compare_fusion
  7.2 0.7 subtract_exponential_fusion
  7.9 0.6 fusion.60
  8.5 0.6 exp.41
  9.0 1.3 multiply_bitcast_fusion
  10.4 0.0 copy-start
  10.4 0.0 collective-permute-done.1.after_ref
  10.4 0.7 copy-done
  11.1 0.7 copy-done.1
  11.8 8.1 %shard_map.28 = (f32[5,32,64,128]{3,2,1,0:T(8,128)}, f32[5,2,64,128]{3,2,1,0:T(8,128)}) custom-call(f32[5,32,64,128]{3,2,1,0:T(8,128)} %fields_ref.1, f32[5,2,64,128]{3,2,1,0:T(8,128)} %copy-done, f32[5,2,64,128]{3,2,1,0:T(8,128)} %copy-done.1), custom_call_target="tpu_custom_call" | custom-call | flops 26214400 | bytes 10485760 | tf_op jit(solution)/shard_map/pallas_call | solution.py:136
  19.9 0.9 slice_bitcast_fusion.1
  20.8 3.8 %collective-permute-start.10 = (f32[5,64,128]{2,1,0:T(8,128)S(1)}, f32[5,64,128]{2,1,0:T(8,128)}, u32[]{:S(2)}, u32[]{:S(2)}) collective-permute-start(f32[5,64,128]{2,1,0:T(8,128)S(1)} %slice_bitcast_fusion.1), channel_id=1, source_target_pairs={{0,224},{16,240},{32,0},{48,16},{64,32},{80,48},{96,64},{112,80},{... | collective-permute-start | bytes 491528 | tf_op jit(solution)/shard_map/ppermute | solution.py:103
  24.6 0.4 collective-permute-start.9
  25.0 11.1 %copy.5 = f32[5,32,64,128]{2,1,3,0:T(8,128)} copy(f32[5,32,64,128]{3,2,1,0:T(8,128)} %fields_ref.1) | data formatting | bytes 10485760 | tf_op jit(solution)/shard_map/optimization_barrier | solution.py:169
  36.1 1.8 %multiply_bitcast_fusion.2 = (f32[32,64,128]{2,1,0:T(8,128)S(1)}, f32[32,64,128]{2,1,0:T(8,128)S(1)}) fusion(f32[5,32,64,128]{3,2,1,0:T(8,128)} %fields_ref.1), kind=kLoop, calls=%fused_computation.44 | loop fusion | flops 524288 | bytes 4194304 | tf_op jit(solution)/shard_map/mul | solution.py:171
  37.9 1.1 fusion.76
  39.0 3.1 %collective-permute-start.2 = (f32[5,32,64,3]{2,1,3,0:T(8,128)S(1)}, f32[5,32,64,3]{2,1,3,0:T(8,128)S(1)}, u32[]{:S(2)}, u32[]{:S(2)}) collective-permute-start(f32[5,32,64,3]{2,1,3,0:T(8,128)S(1)} %get-tuple-element.25), channel_id=1, source_target_pairs={{1,0},{2,1},{3,2},{0,3},{5,4},{6,5},{7,6},{4,7},{9,8},{10,9},{11,1... | collective-permute-start | bytes 368648 | tf_op jit(solution)/shard_map/ppermute | solution.py:23
  42.1 0.0 collective-permute-start.3
  42.1 0.7 slice_bitcast_fusion
  42.8 4.8 %collective-permute-done.2 = f32[5,32,64,3]{2,1,3,0:T(8,128)S(1)} collective-permute-done((f32[5,32,64,3]{2,1,3,0:T(8,128)S(1)}, f32[5,32,64,3]{2,1,3,0:T(8,128)S(1)}, u32[]{:S(2)}, u32[]{:S(2)}) %collective-permute-start.2) | collective-permute-done | bytes 122912 | tf_op jit(solution)/shard_map/ppermute | solution.py:23
  47.6 0.7 copy-done.3
  48.3 4.1 %copy.6 = f32[5,32,64,3]{3,2,1,0:T(8,128)} copy(f32[5,32,64,3]{2,1,3,0:T(8,128)} %copy-done.3) | data formatting | bytes 245760 | tf_op jit(solution)/shard_map/ppermute | solution.py:23
  52.3 4.1 %copy.8 = f32[5,32,64,3]{3,2,1,0:T(8,128)} copy(f32[5,32,64,3]{2,1,3,0:T(8,128)} %collective-permute-done.3) | data formatting | bytes 245760 | tf_op jit(solution)/shard_map/ppermute | solution.py:22
  56.4 29.3 %fusion.6 = f32[5,32,64,128]{3,2,1,0:T(8,128)S(1)} fusion(f32[5,32,64,3]{3,2,1,0:T(8,128)} %copy.8, f32[5,32,64,128]{3,2,1,0:T(8,128)} %fields_ref.1, f32[5,32,64,3]{3,2,1,0:T(8,128)} %copy.6, f32[5,32,64,128]{3,2,1,0:T(8,128)} %get-tuple-element.14, f32[32,64,128]{2,1,0:T(8,128)S(1)} %get-tuple-element.28, f32[32,64,128]{2,1,0:T(8,128)S(1)} %get-tuple-element.27), kind=kLoop, calls=%fused_computation.14 | loop fusion | flops 22282240 | bytes 18071552 | tf_op jit(solution)/shard_map/sub | solution.py:171
  85.8 1.0 multiply_add_fusion.4
  86.8 2.4 %collective-permute-start.11 = (f32[5,64,128]{2,1,0:T(8,128)S(1)}, f32[5,64,128]{2,1,0:T(8,128)S(1)}, u32[]{:S(2)}, u32[]{:S(2)}) collective-permute-start(f32[5,64,128]{2,1,0:T(8,128)S(1)} %multiply_add_fusion.4), channel_id=1, source_target_pairs={{0,224},{16,240},{32,0},{48,16},{64,32},{80,48},{96,64},{112,80},{... | collective-permute-start | bytes 491528 | tf_op jit(solution)/shard_map/ppermute | solution.py:103
  89.2 1.0 multiply_add_fusion.8
  90.2 0.3 collective-permute-start.6
  90.4 2.0 %collective-permute-done.11 = f32[5,64,128]{2,1,0:T(8,128)S(1)} collective-permute-done((f32[5,64,128]{2,1,0:T(8,128)S(1)}, f32[5,64,128]{2,1,0:T(8,128)S(1)}, u32[]{:S(2)}, u32[]{:S(2)}) %collective-permute-start.11) | collective-permute-done | bytes 163872 | tf_op jit(solution)/shard_map/ppermute | solution.py:103
  92.5 6.2 %collective-permute-start.12 = (f32[5,64,128]{2,1,0:T(8,128)S(1)}, f32[5,64,128]{2,1,0:T(8,128)S(1)}, u32[]{:S(2)}, u32[]{:S(2)}) collective-permute-start(f32[5,64,128]{2,1,0:T(8,128)S(1)} %multiply_add_fusion.3), channel_id=1, source_target_pairs={{0,192},{16,208},{32,224},{48,240},{64,0},{80,16},{96,32},{112,48}... | collective-permute-start | bytes 491528 | tf_op jit(solution)/shard_map/ppermute | solution.py:103
  98.6 0.1 collective-permute-start.7
  98.7 5.3 %collective-permute-done.12 = f32[5,64,128]{2,1,0:T(8,128)S(1)} collective-permute-done((f32[5,64,128]{2,1,0:T(8,128)S(1)}, f32[5,64,128]{2,1,0:T(8,128)S(1)}, u32[]{:S(2)}, u32[]{:S(2)}) %collective-permute-start.12) | collective-permute-done | bytes 163872 | tf_op jit(solution)/shard_map/ppermute | solution.py:103
  104.0 3.5 %collective-permute-start.13 = (f32[5,64,128]{2,1,0:T(8,128)S(1)}, f32[5,64,128]{2,1,0:T(8,128)S(1)}, u32[]{:S(2)}, u32[]{:S(2)}) collective-permute-start(f32[5,64,128]{2,1,0:T(8,128)S(1)} %multiply_add_fusion.2), channel_id=1, source_target_pairs={{0,128},{16,144},{32,160},{48,176},{64,192},{80,208},{96,224},{112... | collective-permute-start | bytes 491528 | tf_op jit(solution)/shard_map/ppermute | solution.py:103
  107.5 15.1 %collective-permute-done.7 = f32[5,64,128]{2,1,0:T(8,128)S(1)} collective-permute-done((f32[5,64,128]{2,1,0:T(8,128)S(1)}, f32[5,64,128]{2,1,0:T(8,128)S(1)}, u32[]{:S(2)}, u32[]{:S(2)}) %collective-permute-start.7) | collective-permute-done | bytes 163872 | tf_op jit(solution)/shard_map/ppermute | solution.py:103
  122.7 2.3 %collective-permute-start.8 = (f32[5,64,128]{2,1,0:T(8,128)S(1)}, f32[5,64,128]{2,1,0:T(8,128)S(1)}, u32[]{:S(2)}, u32[]{:S(2)}) collective-permute-start(f32[5,64,128]{2,1,0:T(8,128)S(1)} %multiply_add_fusion.6), channel_id=1, source_target_pairs={{0,128},{16,144},{32,160},{48,176},{64,192},{80,208},{96,224},{112... | collective-permute-start | bytes 491528 | tf_op jit(solution)/shard_map/ppermute | solution.py:103
  125.0 7.0 %collective-permute-done.8 = f32[5,64,128]{2,1,0:T(8,128)S(1)} collective-permute-done((f32[5,64,128]{2,1,0:T(8,128)S(1)}, f32[5,64,128]{2,1,0:T(8,128)S(1)}, u32[]{:S(2)}, u32[]{:S(2)}) %collective-permute-start.8) | collective-permute-done | bytes 163872 | tf_op jit(solution)/shard_map/ppermute | solution.py:103
  132.1 6.3 %fusion.29 = f32[5,32,64,128]{3,2,1,0:T(8,128)S(1)} fusion(f32[5,32,64,128]{3,2,1,0:T(8,128)S(1)} %fusion.6, f32[32,64,128]{2,1,0:T(8,128)S(1)} %multiply_bitcast_fusion, f32[5,64,128]{2,1,0:T(8,128)S(1)} %multiply_add_fusion.1, f32[32]{0:T(128)S(1)} %copy-done.15, f32[5,64,128]{2,1,0:T(8,128)S(1)} %multiply_add_fusion.5, f32[32]{0:T(128)S(1)} %copy-done.14, ...), kind=kOutput, calls=%fused_computation.40 | convolution fusion | flops 1013268480 | bytes 11868928 | tf_op jit(solution)/shard_map/fik,fxkz->fxiz/dot_general | solution.py:90
  138.4 0.1 slice.91
  138.5 3.4 %collective-permute-start.14 = (f32[5,32,128]{2,1,0:T(8,128)S(1)}, f32[5,32,128]{2,1,0:T(8,128)S(1)}, u32[]{:S(2)}, u32[]{:S(2)}) collective-permute-start(f32[5,32,128]{2,1,0:T(8,128)S(1)} %bitcast.50), channel_id=1, source_target_pairs={{0,4},{4,8},{8,12},{1,5},{5,9},{9,13},{2,6},{6,10},{10,14},{3,7},{... | collective-permute-start | bytes 245768 | tf_op jit(solution)/shard_map/ppermute | solution.py:63
  141.9 4.6 %collective-permute-start.15 = (f32[5,32,128]{2,1,0:T(8,128)S(1)}, f32[5,32,128]{2,1,0:T(8,128)S(1)}, u32[]{:S(2)}, u32[]{:S(2)}) collective-permute-start(f32[5,32,128]{2,1,0:T(8,128)S(1)} %bitcast.51), channel_id=1, source_target_pairs={{0,8},{4,12},{1,9},{5,13},{2,10},{6,14},{3,11},{7,15},{16,24},{20,... | collective-permute-start | bytes 245768 | tf_op jit(solution)/shard_map/ppermute | solution.py:63
  146.5 1.5 collective-permute-start.16
  148.1 0.5 collective-permute-done.15
  148.6 1.3 collective-permute-done.16
  149.9 0.1 multiply_add_fusion.10
  150.0 5.9 %fusion.32 = f32[5,32,64,128]{3,2,1,0:T(8,128)S(1)} fusion(f32[5,32,64,128]{3,2,1,0:T(8,128)S(1)} %fusion.29, f32[5,32,128]{2,1,0:T(8,128)S(1)} %multiply_add_fusion.10, f32[5,64]{1,0:T(8,128)S(1)} %copy-done.11, f32[5,64]{1,0:T(8,128)S(1)} %copy-done.10, f32[5,64]{1,0:T(8,128)S(1)} %copy-done.8, pred[64,64]{1,0:T(8,128)(4,1)S(1)} %copy-done.6), kind=kOutput, calls=%fused_computation.41 | convolution fusion | flops 1009315840 | bytes 10575616 | tf_op jit(solution)/shard_map/fik,fxkz->fxiz/dot_general | solution.py:95
  155.9 0.1 slice.92
  156.0 1.3 collective-permute-start.17
  157.3 1.3 collective-permute-start.18
  158.6 1.3 collective-permute-start.19
  159.9 2.4 %collective-permute-done.17 = f32[5,32,128]{2,1,0:T(8,128)S(1)} collective-permute-done((f32[5,32,128]{2,1,0:T(8,128)S(1)}, f32[5,32,128]{2,1,0:T(8,128)S(1)}, u32[]{:S(2)}, u32[]{:S(2)}) %collective-permute-start.17) | collective-permute-done | bytes 81952 | tf_op jit(solution)/shard_map/ppermute | solution.py:63
  162.3 2.8 %collective-permute-done.18 = f32[5,32,128]{2,1,0:T(8,128)S(1)} collective-permute-done((f32[5,32,128]{2,1,0:T(8,128)S(1)}, f32[5,32,128]{2,1,0:T(8,128)S(1)}, u32[]{:S(2)}, u32[]{:S(2)}) %collective-permute-start.18) | collective-permute-done | bytes 81952 | tf_op jit(solution)/shard_map/ppermute | solution.py:63
  165.1 3.1 %collective-permute-done.19 = f32[5,32,128]{2,1,0:T(8,128)S(1)} collective-permute-done((f32[5,32,128]{2,1,0:T(8,128)S(1)}, f32[5,32,128]{2,1,0:T(8,128)S(1)}, u32[]{:S(2)}, u32[]{:S(2)}) %collective-permute-start.19) | collective-permute-done | bytes 81952 | tf_op jit(solution)/shard_map/ppermute | solution.py:63
  168.2 0.1 multiply_add_fusion.9
  168.3 3.3 %multiply_add_fusion = f32[5,32,64,128]{3,2,1,0:T(8,128)} fusion(f32[5,32,64,128]{3,2,1,0:T(8,128)S(1)} %fusion.32, f32[5,32,128]{2,1,0:T(8,128)S(1)} %multiply_add_fusion.9, f32[5,64]{1,0:T(8,128)S(1)} %copy-done.9), kind=kLoop, calls=%fused_computation.23 | loop fusion | flops 2621440 | bytes 10568960 | tf_op jit(solution)/shard_map/add | solution.py:98
  (48 shorter events, 0.2 us)
Async XLA Ops:
  1.1 9.3 %collective-permute-start = (f32[5,2,64,128]{3,2,1,0:T(8,128)S(1)}, f32[5,2,64,128]{3,2,1,0:T(8,128)S(1)}, u32[]{:S(2)}, u32[]{:S(2)}) collective-permute-start(f32[5,2,64,128]{3,2,1,0:T(8,128)S(1)} %get-tuple-element.30), channel_id=1, source_target_pairs={{0,16},{16,32},{32,48},{48,64},{64,80},{80,96},{96,112},{112,128},... | collective-permute-start | bytes 983048 | tf_op jit(solution)/shard_map/ppermute | solution.py:103
  1.1 9.3 %collective-permute-start.1 = (f32[5,2,64,128]{3,2,1,0:T(8,128)S(1)}, f32[5,2,64,128]{3,2,1,0:T(8,128)S(1)}, u32[]{:S(2)}, u32[]{:S(2)}) collective-permute-start(f32[5,2,64,128]{3,2,1,0:T(8,128)S(1)} %get-tuple-element.29), channel_id=1, source_target_pairs={{0,240},{16,0},{32,16},{48,32},{64,48},{80,64},{96,80},{112,96},{1... | collective-permute-start | bytes 983048 | tf_op jit(solution)/shard_map/ppermute | solution.py:103
  5.8 19.2 %copy-start.4 = (f32[5,64]{1,0:T(8,128)}, f32[5,64]{1,0:T(8,128)S(1)}, u32[]{:S(2)}) copy-start(f32[5,64]{1,0:T(8,128)S(1)} %reduce_window_sum.13) | copy-start | bytes 3844
  10.4 0.7 copy-start
  11.1 0.7 copy-start.1
  20.8 64.9 %collective-permute-start.10 = (f32[5,64,128]{2,1,0:T(8,128)S(1)}, f32[5,64,128]{2,1,0:T(8,128)}, u32[]{:S(2)}, u32[]{:S(2)}) collective-permute-start(f32[5,64,128]{2,1,0:T(8,128)S(1)} %slice_bitcast_fusion.1), channel_id=1, source_target_pairs={{0,224},{16,240},{32,0},{48,16},{64,32},{80,48},{96,64},{112,80},{... | collective-permute-start | bytes 491528 | tf_op jit(solution)/shard_map/ppermute | solution.py:103
  24.6 61.2 %collective-permute-start.9 = (f32[5,64,128]{2,1,0:T(8,128)S(1)}, f32[5,64,128]{2,1,0:T(8,128)}, u32[]{:S(2)}, u32[]{:S(2)}) collective-permute-start(f32[5,64,128]{2,1,0:T(8,128)S(1)} %slice_bitcast_fusion.1), channel_id=1, source_target_pairs={{0,240},{16,0},{32,16},{48,32},{64,48},{80,64},{96,80},{112,96},{1... | collective-permute-start | bytes 491528 | tf_op jit(solution)/shard_map/ppermute | solution.py:103
  36.1 6.0 %copy-start.2 = (f32[5,2,64,128]{3,2,1,0:T(8,128)S(1)}, f32[5,2,64,128]{3,2,1,0:T(8,128)}, u32[]{:S(2)}) copy-start(f32[5,2,64,128]{3,2,1,0:T(8,128)} %get-tuple-element.15) | copy-start | bytes 983044
  39.0 8.6 %collective-permute-start.2 = (f32[5,32,64,3]{2,1,3,0:T(8,128)S(1)}, f32[5,32,64,3]{2,1,3,0:T(8,128)S(1)}, u32[]{:S(2)}, u32[]{:S(2)}) collective-permute-start(f32[5,32,64,3]{2,1,3,0:T(8,128)S(1)} %get-tuple-element.25), channel_id=1, source_target_pairs={{1,0},{2,1},{3,2},{0,3},{5,4},{6,5},{7,6},{4,7},{9,8},{10,9},{11,1... | collective-permute-start | bytes 368648 | tf_op jit(solution)/shard_map/ppermute | solution.py:23
  42.1 10.3 %collective-permute-start.3 = (f32[5,32,64,3]{2,1,3,0:T(8,128)S(1)}, f32[5,32,64,3]{2,1,3,0:T(8,128)}, u32[]{:S(2)}, u32[]{:S(2)}) collective-permute-start(f32[5,32,64,3]{2,1,3,0:T(8,128)S(1)} %get-tuple-element.26), channel_id=1, source_target_pairs={{0,1},{1,2},{2,3},{3,0},{4,5},{5,6},{6,7},{7,4},{8,9},{9,10},{10,1... | collective-permute-start | bytes 368648 | tf_op jit(solution)/shard_map/ppermute | solution.py:22
  42.8 46.4 %collective-permute-start.4 = (f32[5,64,128]{2,1,0:T(8,128)}, f32[5,64,128]{2,1,0:T(8,128)}, u32[]{:S(2)}, u32[]{:S(2)}) collective-permute-start(f32[5,64,128]{2,1,0:T(8,128)} %slice_bitcast_fusion), channel_id=1, source_target_pairs={{0,16},{16,32},{32,48},{48,64},{64,80},{80,96},{96,112},{112,128},... | collective-permute-start | bytes 491528 | tf_op jit(solution)/shard_map/ppermute | solution.py:103
  47.6 0.7 copy-start.3
  48.3 40.9 %collective-permute-start.5 = (f32[5,64,128]{2,1,0:T(8,128)}, f32[5,64,128]{2,1,0:T(8,128)}, u32[]{:S(2)}, u32[]{:S(2)}) collective-permute-start(f32[5,64,128]{2,1,0:T(8,128)} %slice_bitcast_fusion), channel_id=1, source_target_pairs={{0,32},{16,48},{32,64},{48,80},{64,96},{80,112},{96,128},{112,144}... | collective-permute-start | bytes 491528 | tf_op jit(solution)/shard_map/ppermute | solution.py:103
  56.4 75.6 %copy-start.5 = (f32[5,64]{1,0:T(8,128)S(1)}, f32[5,64]{1,0:T(8,128)}, u32[]{:S(2)}) copy-start(f32[5,64]{1,0:T(8,128)} %copy-done.4) | copy-start | bytes 3844
  56.4 75.6 %copy-start.7 = (pred[64,64]{1,0:T(8,128)(4,1)S(1)}, pred[64,64]{1,0:T(8,128)(4,1)}, u32[]{:S(2)}) copy-start(pred[64,64]{1,0:T(8,128)(4,1)} %iota_compare_fusion.1) | copy-start | bytes 12292
  56.4 75.6 %copy-start.12 = (f32[5,64]{1,0:T(8,128)S(1)}, f32[5,64]{1,0:T(8,128)}, u32[]{:S(2)}) copy-start(f32[5,64]{1,0:T(8,128)} %get-tuple-element.39) | copy-start | bytes 3844
  56.4 75.6 %copy-start.14 = (f32[32]{0:T(128)S(1)}, f32[32]{0:T(128)}, u32[]{:S(2)}) copy-start(f32[32]{0:T(128)} %get-tuple-element.41) | copy-start | bytes 388
  56.4 75.6 %copy-start.15 = (f32[32]{0:T(128)S(1)}, f32[32]{0:T(128)}, u32[]{:S(2)}) copy-start(f32[32]{0:T(128)} %get-tuple-element.42) | copy-start | bytes 388
  86.8 5.6 %collective-permute-start.11 = (f32[5,64,128]{2,1,0:T(8,128)S(1)}, f32[5,64,128]{2,1,0:T(8,128)S(1)}, u32[]{:S(2)}, u32[]{:S(2)}) collective-permute-start(f32[5,64,128]{2,1,0:T(8,128)S(1)} %multiply_add_fusion.4), channel_id=1, source_target_pairs={{0,224},{16,240},{32,0},{48,16},{64,32},{80,48},{96,64},{112,80},{... | collective-permute-start | bytes 491528 | tf_op jit(solution)/shard_map/ppermute | solution.py:103
  90.2 8.4 %collective-permute-start.6 = (f32[5,64,128]{2,1,0:T(8,128)S(1)}, f32[5,64,128]{2,1,0:T(8,128)S(1)}, u32[]{:S(2)}, u32[]{:S(2)}) collective-permute-start(f32[5,64,128]{2,1,0:T(8,128)S(1)} %multiply_add_fusion.8), channel_id=1, source_target_pairs={{0,32},{16,48},{32,64},{48,80},{64,96},{80,112},{96,128},{112,144}... | collective-permute-start | bytes 491528 | tf_op jit(solution)/shard_map/ppermute | solution.py:103
  92.5 11.6 %collective-permute-start.12 = (f32[5,64,128]{2,1,0:T(8,128)S(1)}, f32[5,64,128]{2,1,0:T(8,128)S(1)}, u32[]{:S(2)}, u32[]{:S(2)}) collective-permute-start(f32[5,64,128]{2,1,0:T(8,128)S(1)} %multiply_add_fusion.3), channel_id=1, source_target_pairs={{0,192},{16,208},{32,224},{48,240},{64,0},{80,16},{96,32},{112,48}... | collective-permute-start | bytes 491528 | tf_op jit(solution)/shard_map/ppermute | solution.py:103
  98.6 24.0 %collective-permute-start.7 = (f32[5,64,128]{2,1,0:T(8,128)S(1)}, f32[5,64,128]{2,1,0:T(8,128)S(1)}, u32[]{:S(2)}, u32[]{:S(2)}) collective-permute-start(f32[5,64,128]{2,1,0:T(8,128)S(1)} %multiply_add_fusion.7), channel_id=1, source_target_pairs={{0,64},{16,80},{32,96},{48,112},{64,128},{80,144},{96,160},{112,17... | collective-permute-start | bytes 491528 | tf_op jit(solution)/shard_map/ppermute | solution.py:103
  104.0 20.9 %collective-permute-start.13 = (f32[5,64,128]{2,1,0:T(8,128)S(1)}, f32[5,64,128]{2,1,0:T(8,128)S(1)}, u32[]{:S(2)}, u32[]{:S(2)}) collective-permute-start(f32[5,64,128]{2,1,0:T(8,128)S(1)} %multiply_add_fusion.2), channel_id=1, source_target_pairs={{0,128},{16,144},{32,160},{48,176},{64,192},{80,208},{96,224},{112... | collective-permute-start | bytes 491528 | tf_op jit(solution)/shard_map/ppermute | solution.py:103
  122.7 9.3 %collective-permute-start.8 = (f32[5,64,128]{2,1,0:T(8,128)S(1)}, f32[5,64,128]{2,1,0:T(8,128)S(1)}, u32[]{:S(2)}, u32[]{:S(2)}) collective-permute-start(f32[5,64,128]{2,1,0:T(8,128)S(1)} %multiply_add_fusion.6), channel_id=1, source_target_pairs={{0,128},{16,144},{32,160},{48,176},{64,192},{80,208},{96,224},{112... | collective-permute-start | bytes 491528 | tf_op jit(solution)/shard_map/ppermute | solution.py:103
  132.0 16.0 %copy-start.13 = (f32[5,4]{0,1:T(4,128)S(1)}, f32[5,4]{0,1:T(4,128)}, u32[]{:S(2)}) copy-start(f32[5,4]{0,1:T(4,128)} %exp.41) | copy-start | bytes 244
  132.1 17.9 %copy-start.6 = (pred[64,64]{1,0:T(8,128)(4,1)S(1)}, pred[64,64]{1,0:T(8,128)(4,1)}, u32[]{:S(2)}) copy-start(pred[64,64]{1,0:T(8,128)(4,1)} %iota_compare_fusion) | copy-start | bytes 12292
  132.1 17.9 %copy-start.8 = (f32[5,64]{1,0:T(8,128)S(1)}, f32[5,64]{1,0:T(8,128)}, u32[]{:S(2)}) copy-start(f32[5,64]{1,0:T(8,128)} %fusion.55) | copy-start | bytes 3844
  132.1 17.9 %copy-start.10 = (f32[5,64]{1,0:T(8,128)S(1)}, f32[5,64]{1,0:T(8,128)}, u32[]{:S(2)}) copy-start(f32[5,64]{1,0:T(8,128)} %get-tuple-element.20) | copy-start | bytes 3844
  132.1 17.9 %copy-start.11 = (f32[5,64]{1,0:T(8,128)S(1)}, f32[5,64]{1,0:T(8,128)}, u32[]{:S(2)}) copy-start(f32[5,64]{1,0:T(8,128)} %get-tuple-element.34) | copy-start | bytes 3844
  138.5 9.6 %collective-permute-start.14 = (f32[5,32,128]{2,1,0:T(8,128)S(1)}, f32[5,32,128]{2,1,0:T(8,128)S(1)}, u32[]{:S(2)}, u32[]{:S(2)}) collective-permute-start(f32[5,32,128]{2,1,0:T(8,128)S(1)} %bitcast.50), channel_id=1, source_target_pairs={{0,4},{4,8},{8,12},{1,5},{5,9},{9,13},{2,6},{6,10},{10,14},{3,7},{... | collective-permute-start | bytes 245768 | tf_op jit(solution)/shard_map/ppermute | solution.py:63
  141.9 6.7 %collective-permute-start.15 = (f32[5,32,128]{2,1,0:T(8,128)S(1)}, f32[5,32,128]{2,1,0:T(8,128)S(1)}, u32[]{:S(2)}, u32[]{:S(2)}) collective-permute-start(f32[5,32,128]{2,1,0:T(8,128)S(1)} %bitcast.51), channel_id=1, source_target_pairs={{0,8},{4,12},{1,9},{5,13},{2,10},{6,14},{3,11},{7,15},{16,24},{20,... | collective-permute-start | bytes 245768 | tf_op jit(solution)/shard_map/ppermute | solution.py:63
  146.5 3.3 %collective-permute-start.16 = (f32[5,32,128]{2,1,0:T(8,128)S(1)}, f32[5,32,128]{2,1,0:T(8,128)S(1)}, u32[]{:S(2)}, u32[]{:S(2)}) collective-permute-start(f32[5,32,128]{2,1,0:T(8,128)S(1)} %bitcast.52), channel_id=1, source_target_pairs={{0,12},{1,13},{2,14},{3,15},{16,28},{17,29},{18,30},{19,31},{32,44... | collective-permute-start | bytes 245768 | tf_op jit(solution)/shard_map/ppermute | solution.py:63
  150.0 18.3 %copy-start.9 = (f32[5,64]{1,0:T(8,128)S(1)}, f32[5,64]{1,0:T(8,128)}, u32[]{:S(2)}) copy-start(f32[5,64]{1,0:T(8,128)} %get-tuple-element.19) | copy-start | bytes 3844
  156.0 6.3 %collective-permute-start.17 = (f32[5,32,128]{2,1,0:T(8,128)S(1)}, f32[5,32,128]{2,1,0:T(8,128)S(1)}, u32[]{:S(2)}, u32[]{:S(2)}) collective-permute-start(f32[5,32,128]{2,1,0:T(8,128)S(1)} %bitcast.53), channel_id=1, source_target_pairs={{4,0},{8,4},{12,8},{5,1},{9,5},{13,9},{6,2},{10,6},{14,10},{7,3},{... | collective-permute-start | bytes 245768 | tf_op jit(solution)/shard_map/ppermute | solution.py:63
  157.3 7.8 %collective-permute-start.18 = (f32[5,32,128]{2,1,0:T(8,128)S(1)}, f32[5,32,128]{2,1,0:T(8,128)S(1)}, u32[]{:S(2)}, u32[]{:S(2)}) collective-permute-start(f32[5,32,128]{2,1,0:T(8,128)S(1)} %bitcast.54), channel_id=1, source_target_pairs={{8,0},{12,4},{9,1},{13,5},{10,2},{14,6},{11,3},{15,7},{24,16},{28,... | collective-permute-start | bytes 245768 | tf_op jit(solution)/shard_map/ppermute | solution.py:63
  158.6 9.6 %collective-permute-start.19 = (f32[5,32,128]{2,1,0:T(8,128)S(1)}, f32[5,32,128]{2,1,0:T(8,128)S(1)}, u32[]{:S(2)}, u32[]{:S(2)}) collective-permute-start(f32[5,32,128]{2,1,0:T(8,128)S(1)} %bitcast.55), channel_id=1, source_target_pairs={{12,0},{13,1},{14,2},{15,3},{28,16},{29,17},{30,18},{31,19},{44,32... | collective-permute-start | bytes 245768 | tf_op jit(solution)/shard_map/ppermute | solution.py:63
